TPU v7x, 32 devices: a whole 2x2x4 slice. The times are simulated.
32 devices in a mesh: node: 8 (over y, x, core), feat: 4 (over z).
Axes of the slice: x: 2, y: 2, z: 4, core: 2. Of those that a mesh axis runs over, the one named last changes fastest.
Arguments:
- features: bfloat16 [8192, 512], P('node', 'feat'), may hold values from -6 to 6
- tiles: bfloat16 [512, 128, 128], P('node'), may hold values from -0.1875 to 0.1875
- block_row: int32 [512], P('node'), may hold values from 0 to 7
- block_col: int32 [512], P('node'), may hold values from 0 to 15, as said below
- block_rel: int32 [512], P('node'), may hold values from 0 to 255
- send_list: int32 [64, 1], P('node'), may hold values from 0 to 7
- coef: float32 [256, 30], replicated, may hold values from -1 to 1
- bases: bfloat16 [30, 512, 512], P(None, 'feat'), may hold values from -0.25 to 0.25
- self_weight: bfloat16 [512, 512], P('feat'), may hold values from -0.25 to 0.25
- cotangent: bfloat16 [8192, 512], P('node', 'feat'), may hold values from -6 to 6
Outputs:
- layer_out: bfloat16 [8192, 512], P('node', 'feat')
- feature_grad: float32 [8192, 512], P('node', 'feat')
- basis_grad: bfloat16 [30, 512, 512], P(None, 'feat')
Inputs may be any that keep to these rules, and one draw needn't show every extreme that they name: `block_col`: each partition's 64 blocks name each of its 16 slots at least once. `send_list`: row p * 8 + q names local blocks of partition p.
All inputs are finite; a program needn't handle non-finite values.
Results may differ from a plain program's by a relative error of at most 0.005.
Values may be sent and summed in bfloat16 or wider, within the bound.
No kernel may reach another device: no remote copies, remote signals or barrier semaphores. Data moves between devices by JAX's collectives and lax.ppermute only.
A program may use at most 64 MiB of HBM per device.

v0:
```python
import math

import jax
import jax.numpy as jnp
from jax import lax
from jax.sharding import PartitionSpec as P


def body(
    features, tiles, block_row, block_col, block_rel, send_list, coef, bases, self_weight, cotangent
):
    exact_products = lax.Precision.HIGHEST
    blk_size = tiles.shape[1]
    owned_blocks = features.shape[0] // blk_size
    col_width = features.shape[1]
    partitions = lax.axis_size("node")
    per_peer = send_list.shape[1]
    full_width = bases.shape[2]
    relations = coef.shape[0]
    node_count = owned_blocks * blk_size
    own_cols = jnp.transpose(features.reshape(owned_blocks, blk_size, col_width), (0, 2, 1))
    outgoing = own_cols[send_list]
    remote_rows = lax.all_to_all(outgoing, "node", split_axis=0, concat_axis=0, tiled=True).reshape(
        partitions * per_peer, col_width, blk_size
    )
    slot_rows = jnp.concatenate([own_cols, remote_rows], axis=0)
    slot_count_total = slot_rows.shape[0]
    source = slot_rows[block_col]
    message = jnp.einsum("kab,kcb->kca", tiles, source, preferred_element_type=jnp.float32)
    row_select = (block_row[:, None] == jnp.arange(owned_blocks, dtype=jnp.int32)[None, :]).astype(
        jnp.float32
    )
    rel_select = (block_rel[:, None] == jnp.arange(relations, dtype=jnp.int32)[None, :]).astype(
        jnp.float32
    )
    block_coef = jnp.dot(rel_select, coef, precision=exact_products)
    summed = jnp.einsum(
        "ki,kb,kca->bica", row_select, block_coef, message, precision=exact_products
    ).astype(jnp.bfloat16)
    scale_factor = 1.0 / math.sqrt(partitions * node_count)
    grad_full = lax.all_gather(cotangent, "feat", axis=1, tiled=True).reshape(
        owned_blocks, blk_size, full_width
    )
    basis_part = jnp.einsum("bica,iae->bce", summed, grad_full, preferred_element_type=jnp.float32)
    basis_total = lax.psum(basis_part * scale_factor, "node")
    basis_grad = basis_total.astype(jnp.bfloat16)
    combined = jnp.einsum("bica,bco->oia", summed, bases, preferred_element_type=jnp.float32)
    feat_parts = lax.axis_size("feat")
    out_cols = full_width // feat_parts
    combined = combined.reshape(feat_parts, out_cols, node_count) + jnp.einsum(
        "nc,co->on", features, self_weight, preferred_element_type=jnp.float32
    ).reshape(feat_parts, out_cols, node_count)
    feat_pos = lax.axis_index("feat")
    layer_cols = jnp.take(combined, feat_pos, axis=0)
    for shift in range(1, feat_parts):
        piece = jnp.take(combined, (feat_pos + shift) % feat_parts, axis=0)
        layer_cols = layer_cols + lax.ppermute(
            piece, "feat", [(g, (g + shift) % feat_parts) for g in range(feat_parts)]
        )
    layer_out = jnp.transpose(layer_cols).astype(jnp.bfloat16)
    grad_summed = jnp.einsum("iae,bce->bica", grad_full, bases, preferred_element_type=jnp.float32)
    grad_message = jnp.einsum(
        "ki,kb,bica->kca", row_select, block_coef, grad_summed, precision=exact_products
    ).astype(jnp.bfloat16)
    grad_source = jnp.einsum(
        "kab,kca->kcb", tiles, grad_message, preferred_element_type=jnp.float32
    )
    col_select = (
        block_col[:, None] == jnp.arange(slot_count_total, dtype=jnp.int32)[None, :]
    ).astype(jnp.float32)
    slot_grad = jnp.einsum("ks,kcb->scb", col_select, grad_source, precision=exact_products)
    leaving = slot_grad[owned_blocks:].reshape(partitions, per_peer, col_width, blk_size)
    returned = (
        lax.all_to_all(
            leaving.astype(jnp.bfloat16), "node", split_axis=0, concat_axis=0, tiled=True
        )
        .astype(leaving.dtype)
        .reshape(partitions * per_peer, col_width, blk_size)
    )
    send_select = (
        send_list.reshape(-1)[:, None] == jnp.arange(owned_blocks, dtype=jnp.int32)[None, :]
    ).astype(jnp.float32)
    arrived = jnp.einsum("ti,tcb->icb", send_select, returned, precision=exact_products)
    own_grad = jnp.transpose(slot_grad[:owned_blocks] + arrived, (0, 2, 1))
    self_loop_gradient = jnp.einsum(
        "iae,ce->iac", grad_full, self_weight, preferred_element_type=jnp.float32
    )
    feature_grad = (own_grad + self_loop_gradient).reshape(node_count, col_width)
    return (layer_out, feature_grad, basis_grad)


def solution(mesh):
    return jax.shard_map(
        body,
        mesh=mesh,
        in_specs=(
            P("node", "feat"),
            P("node", None, None),
            P("node"),
            P("node"),
            P("node"),
            P("node", None),
            P(),
            P(None, "feat", None),
            P("feat", None),
            P("node", "feat"),
        ),
        out_specs=(P("node", "feat"), P("node", "feat"), P(None, "feat", None)),
        check_vma=False,
    )
```

profile of v0, /device:TPU:0, one launch (start us, length us, event | category | flops | bytes accessed | tf_op | source)
XLA Modules:
  0.0 345.6 jit_solution(1916604174697822274)
XLA Ops:
  7.2 0.0 copy-start
  7.2 0.0 all-gather.2.cloned.1.call-start
  7.2 0.7 all-gather.2.cloned.1.call-update
  7.9 0.7 fusion.44
  8.6 0.0 copy-start.11
  8.6 0.0 copy-start.3
  8.6 2.3 gather_fusion
  10.9 5.2 %all-to-all-start = ((bf16[8,1,128,128]{2,3,1,0:T(8,128)(2,1)}), bf16[8,1,128,128]{2,3,1,0:T(8,128)(2,1)S(1)}, u32[]{:S(2)}, u32[]{:S(2)}) async-start(bf16[8,1,128,128]{2,3,1,0:T(8,128)(2,1)} %bitcast.6), calls=%async_computation | async-start | bytes 524288 | tf_op jit(solution)/shard_map/all_to_all | solution.py:23
  16.1 0.7 compare_select_fusion
  16.7 0.7 fusion.40
  17.4 2.8 fusion.46
  20.2 3.0 copy.21
  23.2 0.2 fusion.31
  23.4 0.0 all-to-all-done
  23.5 2.1 gather_fusion.1
  25.6 0.0 copy-done
  25.6 3.2 fusion.45
  28.8 20.4 %convolution_convert_fusion = bf16[30,8,128,128]{3,1,2,0:T(8,128)(2,1)S(1)} fusion(f32[64,128,128]{2,1,0:T(8,128)S(1)} %fusion.45, f32[64,8]{0,1:T(8,128)S(1)} %fusion.40, f32[64,30]{0,1:T(8,128)S(1)} %fusion.31), kind=kOutput, calls=%fused_computation.10 | convolution fusion | flops 3023846400 | bytes 12068352 | tf_op jit(solution)/shard_map/ki,kb,kca->bica/dot_general | solution.py:37
  49.2 3.0 copy-done.2
  52.3 5.6 %fusion.15 = f32[512,8,128]{0,2,1:T(8,128)} fusion(bf16[30,128,512]{2,1,0:T(8,128)(2,1)S(1)} %copy-done.8, bf16[30,8,128,128]{3,1,2,0:T(8,128)(2,1)S(1)} %convolution_convert_fusion), kind=kOutput, calls=%fused_computation.20 | convolution fusion | flops 4026531840 | bytes 13893632 | tf_op jit(solution)/shard_map/bica,bco->oia/dot_general | solution.py:47
  57.8 2.9 reshape.35
  60.7 2.4 copy_add_fusion
  63.2 0.0 copy-start.1
  63.2 1.3 copy-done.1
  64.5 0.9 select_bitcast_fusion.2
  65.4 1.6 collective-permute-start
  67.0 2.2 collective-permute-start.2
  69.2 0.8 collective-permute-start.1
  70.0 12.3 %collective-permute-done = f32[128,1024]{0,1:T(8,128)} collective-permute-done((f32[128,1024]{0,1:T(8,128)}, f32[128,1024]{0,1:T(8,128)}, u32[]{:S(2)}, u32[]{:S(2)}) %collective-permute-start) | collective-permute-done | bytes 524320 | tf_op jit(solution)/shard_map/ppermute | solution.py:57
  82.2 10.1 %collective-permute-done.2 = f32[128,1024]{0,1:T(8,128)} collective-permute-done((f32[128,1024]{0,1:T(8,128)S(1)}, f32[128,1024]{0,1:T(8,128)}, u32[]{:S(2)}, u32[]{:S(2)}) %collective-permute-start.2) | collective-permute-done | bytes 524320 | tf_op jit(solution)/shard_map/ppermute | solution.py:57
  92.4 23.2 %collective-permute-done.1 = f32[128,1024]{0,1:T(8,128)} collective-permute-done((f32[128,1024]{0,1:T(8,128)S(1)}, f32[128,1024]{0,1:T(8,128)}, u32[]{:S(2)}, u32[]{:S(2)}) %collective-permute-start.1) | collective-permute-done | bytes 524320 | tf_op jit(solution)/shard_map/ppermute | solution.py:57
  115.6 2.3 fusion.25
  117.9 8.9 %bitcast_multiply_fusion = f32[30,128,512]{2,1,0:T(8,128)} fusion(bf16[8,128,512,1]{2,1,0,3:T(8,128)(2,1)} %bitcast.96, bf16[30,8,128,128]{3,1,2,0:T(8,128)(2,1)} %copy-done.2), kind=kOutput, calls=%fused_computation.5 | convolution fusion | flops 4028497920 | bytes 16777216 | tf_op jit(solution)/shard_map/bica,iae->bce/dot_general | solution.py:44
  126.8 7.8 %convolution_bitcast_fusion = f32[30,8,128,128]{3,2,1,0:T(8,128)} fusion(bf16[8,128,512,1]{2,1,0,3:T(8,128)(2,1)S(1)} %bitcast.98, bf16[30,128,512]{2,1,0:T(8,128)(2,1)S(1)} %copy-done.9), kind=kOutput, calls=%fused_computation.4 | convolution fusion | flops 4026531840 | bytes 20709376 | tf_op jit(solution)/shard_map/iae,bce->bica/dot_general | solution.py:61
  134.6 159.1 %all-reduce.1 = bf16[30,128,512]{2,1,0:T(8,128)(2,1)} all-reduce(f32[30,128,512]{2,1,0:T(8,128)} %bitcast_multiply_fusion), channel_id=1, replica_groups=mesh['node'=8,'feat'=4] {'node'}, use_global_device_ids=true, to_apply=%region_0.2 | all-reduce | flops 1966080 | bytes 11796480 | tf_op jit(solution)/shard_map/psum | solution.py:45
  293.7 23.9 %fusion = bf16[64,128,128,1]{2,0,3,1:T(8,128)(2,1)S(1)} fusion(f32[30,8,128,128]{3,2,1,0:T(8,128)} %convolution_bitcast_fusion, f32[64,8]{0,1:T(8,128)S(1)} %fusion.40, f32[64,30]{0,1:T(8,128)S(1)} %fusion.31), kind=kOutput, calls=%fused_computation.2 | convolution fusion | flops 3019914240 | bytes 17835520 | tf_op jit(solution)/shard_map/ki,kb,bica->kca/dot_general | solution.py:62
  317.7 0.0 copy-start.7
  317.7 2.0 fusion.14
  319.7 0.0 copy-done.7
  319.7 3.8 %fusion.7 = f32[16,128,128]{2,0,1:T(8,128)S(1)} fusion(f32[64,128,128]{2,1,0:T(8,128)S(1)} %fusion.14, s32[64]{0:T(128)S(1)} %copy-done.7), kind=kOutput, calls=%fused_computation.13 | convolution fusion | flops 201327616 | bytes 5243136 | tf_op jit(solution)/shard_map/ks,kcb->scb/dot_general | solution.py:71
  323.6 0.7 copy.22
  324.4 3.4 all-to-all-start.1
  327.8 2.5 fusion.29
  330.2 2.0 copy.24
  332.3 2.4 all-to-all-done.1
  334.6 0.0 copy-done.6
  334.6 2.1 fusion.21
  336.7 2.0 copy.37
  (19 shorter events, 0.1 us)
Async XLA Ops:
  7.2 18.5 %copy-start = (bf16[64,128,128]{2,1,0:T(8,128)(2,1)S(1)}, bf16[64,128,128]{2,1,0:T(8,128)(2,1)}, u32[]{:S(2)}) copy-start(bf16[64,128,128]{2,1,0:T(8,128)(2,1)} %param.13) | copy-start | bytes 6291460
  7.2 110.7 %all-gather.2.cloned.1.call-start = ((), (), s32[]{:S(2)}) async-start(), calls=%async_computation.2 | async-start | bytes 1310720 | tf_op jit(solution)/shard_map/all_gather | solution.py:41
  8.6 14.6 %copy-start.10 = (f32[256,30]{0,1:T(8,128)S(1)}, f32[256,30]{0,1:T(8,128)}, u32[]{:S(2)}) copy-start(f32[256,30]{0,1:T(8,128)} %param.18) | copy-start | bytes 92164
  8.6 14.6 %copy-start.11 = (s32[64]{0:T(128)S(1)}, s32[64]{0:T(128)}, u32[]{:S(2)}) copy-start(s32[64]{0:T(128)} %param.16) | copy-start | bytes 772
  8.6 14.8 %copy-start.3 = (bf16[1024,128]{1,0:T(8,128)(2,1)S(1)}, bf16[1024,128]{1,0:T(8,128)(2,1)}, u32[]{:S(2)}) copy-start(bf16[1024,128]{1,0:T(8,128)(2,1)} %param.12) | copy-start | bytes 786436
  10.9 12.5 %all-to-all-start = ((bf16[8,1,128,128]{2,3,1,0:T(8,128)(2,1)}), bf16[8,1,128,128]{2,3,1,0:T(8,128)(2,1)S(1)}, u32[]{:S(2)}, u32[]{:S(2)}) async-start(bf16[8,1,128,128]{2,3,1,0:T(8,128)(2,1)} %bitcast.6), calls=%async_computation | async-start | bytes 524288 | tf_op jit(solution)/shard_map/all_to_all | solution.py:23
  28.8 23.4 %copy-start.8 = (bf16[30,128,512]{2,1,0:T(8,128)(2,1)S(1)}, bf16[30,128,512]{2,1,0:T(8,128)(2,1)}, u32[]{:S(2)}) copy-start(bf16[30,128,512]{2,1,0:T(8,128)(2,1)} %param.19) | copy-start | bytes 11796484
  49.2 3.0 copy-start.2
  63.2 1.3 copy-start.1
  65.4 16.9 %collective-permute-start = (f32[128,1024]{0,1:T(8,128)}, f32[128,1024]{0,1:T(8,128)}, u32[]{:S(2)}, u32[]{:S(2)}) collective-permute-start(f32[128,1024]{0,1:T(8,128)} %get-tuple-element.21), channel_id=1, source_target_pairs={{0,1},{1,2},{2,3},{3,0},{4,5},{5,6},{6,7},{7,4},{8,9},{9,10},{10,1... | collective-permute-start | bytes 1572872 | tf_op jit(solution)/shard_map/ppermute | solution.py:57
  67.0 25.4 %collective-permute-start.2 = (f32[128,1024]{0,1:T(8,128)S(1)}, f32[128,1024]{0,1:T(8,128)}, u32[]{:S(2)}, u32[]{:S(2)}) collective-permute-start(f32[128,1024]{0,1:T(8,128)S(1)} %get-tuple-element.22), channel_id=1, source_target_pairs={{0,3},{1,0},{2,1},{3,2},{4,7},{5,4},{6,5},{7,6},{8,11},{9,8},{10,9... | collective-permute-start | bytes 1572872 | tf_op jit(solution)/shard_map/ppermute | solution.py:57
  69.2 46.4 %collective-permute-start.1 = (f32[128,1024]{0,1:T(8,128)S(1)}, f32[128,1024]{0,1:T(8,128)}, u32[]{:S(2)}, u32[]{:S(2)}) collective-permute-start(f32[128,1024]{0,1:T(8,128)S(1)} %get-tuple-element.23), channel_id=1, source_target_pairs={{0,2},{1,3},{2,0},{3,1},{4,6},{5,7},{6,4},{7,5},{8,10},{9,11},{10,... | collective-permute-start | bytes 1572872 | tf_op jit(solution)/shard_map/ppermute | solution.py:57
  117.9 8.9 %copy-start.4 = (bf16[1024,512]{1,0:T(8,128)(2,1)S(1)}, bf16[1024,512]{1,0:T(8,128)(2,1)}, u32[]{:S(2)}) copy-start(bf16[1024,512]{1,0:T(8,128)(2,1)} %all-gather.2.cloned.1.call-done) | copy-start | bytes 3145732
  117.9 8.9 %copy-start.9 = (bf16[30,128,512]{2,1,0:T(8,128)(2,1)S(1)}, bf16[30,128,512]{2,1,0:T(8,128)(2,1)}, u32[]{:S(2)}) copy-start(bf16[30,128,512]{2,1,0:T(8,128)(2,1)} %param.19) | copy-start | bytes 11796484
  317.7 2.1 copy-start.7
  319.7 8.0 %copy-start.5 = (bf16[128,512]{1,0:T(8,128)(2,1)S(1)}, bf16[128,512]{1,0:T(8,128)(2,1)}, u32[]{:S(2)}) copy-start(bf16[128,512]{1,0:T(8,128)(2,1)} %param.20) | copy-start | bytes 393220
  319.7 14.9 %copy-start.6 = (s32[8,1]{0,1:T(1,128)S(1)}, s32[8,1]{0,1:T(1,128)}, u32[]{:S(2)}) copy-start(s32[8,1]{0,1:T(1,128)} %param.17) | copy-start | bytes 100
  324.4 10.3 %all-to-all-start.1 = ((bf16[8,1,128,128]{3,2,1,0:T(8,128)(2,1)}), bf16[8,1,128,128]{3,2,1,0:T(8,128)(2,1)S(1)}, u32[]{:S(2)}, u32[]{:S(2)}) async-start(bf16[8,1,128,128]{3,2,1,0:T(8,128)(2,1)} %copy.22), calls=%async_computation.1 | async-start | bytes 524288 | tf_op jit(solution)/shard_map/all_to_all | solution.py:74
Sparse Core Ops, SparseCore 0:
  9.6 32.8 all-gather.1
where the time goes:
time: 346 us
  blocking collectives  159 us (46%)
  matrix products  83.2 us (24%)
  waiting for transfers between devices  48.7 us (14%)
  local copies, waits for them, and re-layouts  19.5 us (6%)
  between operations  14.2 us (4%)
  starting transfers between devices  13.2 us (4%)
  other arithmetic  7.7 us (2%)
    psum x1, blocking collectives, body(): basis_total = lax.psum(basis_part * scale_factor, 'node')  159 us
    ppermute x3, waiting for transfers between devices, body(): lax.ppermute(piece, 'feat', [(g, (g + shift) % feat_parts) for g in range...  45.6 us
    dot_general x1, matrix products, body(): jnp.einsum('ki,kb,bica->kca', row_select, block_coef, grad_summed, precis...  23.9 us
    dot_general x1, matrix products, body(): jnp.einsum('ki,kb,kca->bica', row_select, block_coef, message, precision=...  20.4 us
    dot_general x1, matrix products, body(): jnp.einsum('bica,iae->bce', summed, grad_full, preferred_element_type=jnp...  8.91 us
    dot_general x1, matrix products, body(): jnp.einsum('iae,bce->bica', grad_full, bases, preferred_element_type=jnp....  7.8 us
  transfers between devices with their start and end apart: 6, of which 4 were waited for; matrix products, arithmetic and copies ran while one was open for 16% of the time, Pallas kernels for 0%

commit v1 on v0

--- a/solution.py
+++ b/solution.py
@@ -42,21 +42,15 @@
         owned_blocks, blk_size, full_width
     )
     basis_part = jnp.einsum("bica,iae->bce", summed, grad_full, preferred_element_type=jnp.float32)
-    basis_total = lax.psum(basis_part * scale_factor, "node")
-    basis_grad = basis_total.astype(jnp.bfloat16)
+    basis_total = lax.psum(basis_part, "node")
+    basis_grad = (basis_total * scale_factor).astype(jnp.bfloat16)
     combined = jnp.einsum("bica,bco->oia", summed, bases, preferred_element_type=jnp.float32)
     feat_parts = lax.axis_size("feat")
     out_cols = full_width // feat_parts
     combined = combined.reshape(feat_parts, out_cols, node_count) + jnp.einsum(
         "nc,co->on", features, self_weight, preferred_element_type=jnp.float32
     ).reshape(feat_parts, out_cols, node_count)
-    feat_pos = lax.axis_index("feat")
-    layer_cols = jnp.take(combined, feat_pos, axis=0)
-    for shift in range(1, feat_parts):
-        piece = jnp.take(combined, (feat_pos + shift) % feat_parts, axis=0)
-        layer_cols = layer_cols + lax.ppermute(
-            piece, "feat", [(g, (g + shift) % feat_parts) for g in range(feat_parts)]
-        )
+    layer_cols = lax.all_to_all(combined, "feat", split_axis=0, concat_axis=0, tiled=True).sum(0)
     layer_out = jnp.transpose(layer_cols).astype(jnp.bfloat16)
     grad_summed = jnp.einsum("iae,bce->bica", grad_full, bases, preferred_element_type=jnp.float32)
     grad_message = jnp.einsum(

time: 346 us -> 219 us (0.63)
  blocking collectives: 159 us -> 0 us
  waiting for transfers between devices: 48.7 us -> 72.3 us
  other arithmetic: 7.7 us -> 14.8 us
    psum x1 -> x0, blocking collectives: 159 us -> none  [body(): basis_total = lax.psum(basis_part * scale_factor, 'node')]
    ppermute x3 -> x0, waiting for transfers between devices: 45.6 us -> none  [body(): lax.ppermute(piece, 'feat', [(g, (g + shift) % feat_parts) for g in range...]
    all_to_all x0 -> x1, waiting for transfers between devices: none -> 37.5 us  [body(): lax.all_to_all(combined, 'feat', split_axis=0, concat_axis=0, tiled=True)]
    psum x0 -> x1, waiting for transfers between devices: none -> 28.1 us  [body(): basis_total = lax.psum(basis_part, 'node')]
    ppermute x3 -> x0, starting transfers between devices: 4.62 us -> none  [body(): lax.ppermute(piece, 'feat', [(g, (g + shift) % feat_parts) for g in range...]
    all_to_all x0 -> x1, starting transfers between devices: none -> 4.6 us  [body(): lax.all_to_all(combined, 'feat', split_axis=0, concat_axis=0, tiled=True)]
    convert_element_type x1, other arithmetic: 2.31 us -> 6.35 us  [body(): basis_grad = (basis_total * scale_factor).astype(jnp.bfloat16)]
    all_to_all x1, waiting for transfers between devices: 2.37 us -> 5.97 us  [body(): lax.all_to_all(leaving.astype(jnp.bfloat16), 'node', split_axis=0, concat...]
  transfers between devices with their start and end apart: 6 -> 5, of which waited for: 4 -> 3; matrix products, arithmetic and copies ran while one was open for 16% -> 41% of each run, Pallas kernels for 0% -> 0%
where the time goes in v1:
time: 219 us; the launch traced here: 218 us
  matrix products  84.5 us (39%)
  waiting for transfers between devices  72.3 us (33%)
  local copies, waits for them, and re-layouts  18.1 us (8%)
  other arithmetic  14.8 us (7%)
  between operations  14.2 us (6%)
  starting transfers between devices  14 us (6%)
    all_to_all x1, waiting for transfers between devices, body(): lax.all_to_all(combined, 'feat', split_axis=0, concat_axis=0, tiled=True)  37.5 us
    psum x1, waiting for transfers between devices, body(): basis_total = lax.psum(basis_part, 'node')  28.1 us
    dot_general x1, matrix products, body(): jnp.einsum('ki,kb,bica->kca', row_select, block_coef, grad_summed, precis...  23.9 us
    dot_general x1, matrix products, body(): jnp.einsum('ki,kb,kca->bica', row_select, block_coef, message, precision=...  20.2 us
    dot_general x1, matrix products, body(): jnp.einsum('iae,bce->bica', grad_full, bases, preferred_element_type=jnp....  9.32 us
    dot_general x1, matrix products, body(): jnp.einsum('bica,iae->bce', summed, grad_full, preferred_element_type=jnp...  8.92 us
    convert_element_type x1, other arithmetic, body(): basis_grad = (basis_total * scale_factor).astype(jnp.bfloat16)  6.35 us
    all_to_all x1, waiting for transfers between devices, body(): lax.all_to_all(leaving.astype(jnp.bfloat16), 'node', split_axis=0, concat...  5.97 us
  transfers between devices with their start and end apart: 5, of which 3 were waited for; matrix products, arithmetic and copies ran while one was open for 41% of the time, Pallas kernels for 0%

profile of v1, /device:TPU:0, one launch (start us, length us, event | category | flops | bytes accessed | tf_op | source)
XLA Modules:
  0.0 218.0 jit_solution(7757608860768085715)
XLA Ops:
  7.2 0.0 copy-start
  7.2 0.0 all-gather.2.cloned.1.call-start
  7.2 0.7 all-gather.2.cloned.1.call-update
  7.9 0.0 copy-start.8
  7.9 0.0 copy-start.9
  7.9 0.0 copy-start.2
  7.9 0.7 fusion.41
  8.7 2.2 %gather_fusion = bf16[8,128,128]{1,2,0:T(8,128)(2,1)} fusion(bf16[8,128,128]{1,2,0:T(8,128)(2,1)} %bitcast.79, s32[1024]{0:T(1024)S(1)} %pad_clamp_fusion.1), kind=kCustom, calls=%fused_computation | custom fusion | bytes 524320 | tf_op jit(solution)/shard_map/gather | solution.py:22
  10.9 5.2 %all-to-all-start = ((bf16[8,1,128,128]{2,3,1,0:T(8,128)(2,1)}), bf16[8,1,128,128]{2,3,1,0:T(8,128)(2,1)S(1)}, u32[]{:S(2)}, u32[]{:S(2)}) async-start(bf16[8,1,128,128]{2,3,1,0:T(8,128)(2,1)} %bitcast.6), calls=%async_computation | async-start | bytes 524288 | tf_op jit(solution)/shard_map/all_to_all | solution.py:23
  16.1 0.0 all-reduce.2.cloned.1.call-start
  16.1 0.7 compare_select_fusion
  16.8 0.7 fusion.37
  17.4 2.8 %fusion.43 = f32[512,1024]{1,0:T(8,128)} fusion(bf16[128,512]{1,0:T(8,128)(2,1)} %param.18, bf16[1024,128]{1,0:T(8,128)(2,1)} %param.10), kind=kOutput, calls=%fused_computation.56 | convolution fusion | flops 134217728 | bytes 2490368 | tf_op jit(solution)/shard_map/nc,co->on/dot_general | solution.py:50
  20.2 2.9 %copy.20 = f32[4,128,1024]{1,2,0:T(8,128)} copy(f32[4,128,1024]{2,1,0:T(8,128)} %bitcast.78) | data formatting | bytes 4194304 | tf_op jit(solution)/shard_map/reshape | solution.py:52
  23.1 0.0 copy-done.8
  23.1 0.0 copy-done.9
  23.1 0.2 fusion.28
  23.4 0.0 all-to-all-done
  23.4 0.0 copy-done.2
  23.5 2.1 gather_fusion.1
  25.6 0.0 copy-done
  25.6 3.2 %fusion.42 = f32[64,128,128]{2,1,0:T(8,128)S(1)} fusion(bf16[64,128,128]{1,2,0:T(8,128)(2,1)} %gather_fusion.1, bf16[64,128,128]{2,1,0:T(8,128)(2,1)S(1)} %copy-done), kind=kOutput, calls=%fused_computation.55 | convolution fusion | flops 268435456 | bytes 8388608 | tf_op jit(solution)/shard_map/kab,kcb->kca/dot_general | solution.py:29
  28.8 20.2 %convolution_convert_fusion = bf16[30,8,128,128]{3,1,2,0:T(8,128)(2,1)S(1)} fusion(f32[64,128,128]{2,1,0:T(8,128)S(1)} %fusion.42, f32[64,8]{0,1:T(8,128)S(1)} %fusion.37, f32[64,30]{0,1:T(8,128)S(1)} %fusion.28), kind=kOutput, calls=%fused_computation.10 | convolution fusion | flops 3023846400 | bytes 12068352 | tf_op jit(solution)/shard_map/ki,kb,kca->bica/dot_general | solution.py:37
  49.0 0.0 copy-start.1
  49.0 3.0 %copy-done.1 = bf16[30,8,128,128]{3,1,2,0:T(8,128)(2,1)} copy-done((bf16[30,8,128,128]{3,1,2,0:T(8,128)(2,1)}, bf16[30,8,128,128]{3,1,2,0:T(8,128)(2,1)S(1)}, u32[]{:S(2)}) %copy-start.1) | copy-done | bytes 7864344
  52.0 0.0 copy-done.7
  52.0 5.6 %fusion.16 = f32[512,8,128]{0,2,1:T(8,128)} fusion(bf16[30,128,512]{2,1,0:T(8,128)(2,1)S(1)} %copy-done.7, bf16[30,8,128,128]{3,1,2,0:T(8,128)(2,1)S(1)} %convolution_convert_fusion), kind=kOutput, calls=%fused_computation.21 | convolution fusion | flops 4026531840 | bytes 13893632 | tf_op jit(solution)/shard_map/bica,bco->oia/dot_general | solution.py:47
  57.6 2.9 %reshape.34 = f32[4,128,1024]{1,0,2:T(4,128)} reshape(f32[512,8,128]{0,2,1:T(8,128)} %fusion.16) | data formatting | bytes 4194304 | tf_op jit(solution)/shard_map/reshape | solution.py:50
  60.5 8.9 %fusion.12 = f32[30,128,512]{2,1,0:T(8,128)} fusion(bf16[8,128,512,1]{2,1,0,3:T(8,128)(2,1)} %bitcast.81, bf16[30,8,128,128]{3,1,2,0:T(8,128)(2,1)} %copy-done.1), kind=kOutput, calls=%fused_computation.18 | convolution fusion | flops 4026531840 | bytes 16777216 | tf_op jit(solution)/shard_map/bica,iae->bce/dot_general | solution.py:44
  69.4 9.3 %convolution_bitcast_fusion = f32[30,8,128,128]{3,2,1,0:T(8,128)} fusion(bf16[8,128,512,1]{2,1,0,3:T(8,128)(2,1)S(1)} %bitcast.83, bf16[30,128,512]{2,1,0:T(8,128)(2,1)} %param.17), kind=kOutput, calls=%fused_computation.4 | convolution fusion | flops 4026531840 | bytes 20709376 | tf_op jit(solution)/shard_map/iae,bce->bica/dot_general | solution.py:55
  78.8 0.0 all-reduce.2.cloned.1.call-update
  78.8 23.9 %fusion = bf16[64,128,128,1]{2,0,3,1:T(8,128)(2,1)S(1)} fusion(f32[30,8,128,128]{3,2,1,0:T(8,128)} %convolution_bitcast_fusion, f32[64,8]{0,1:T(8,128)S(1)} %fusion.37, f32[64,30]{0,1:T(8,128)S(1)} %fusion.28), kind=kOutput, calls=%fused_computation.2 | convolution fusion | flops 3019914240 | bytes 17835520 | tf_op jit(solution)/shard_map/ki,kb,bica->kca/dot_general | solution.py:56
  102.7 0.0 copy-start.6
  102.7 2.0 fusion.15
  104.8 3.8 %fusion.7 = f32[16,128,128]{2,0,1:T(8,128)S(1)} fusion(f32[64,128,128]{2,1,0:T(8,128)S(1)} %fusion.15, s32[64]{0:T(128)S(1)} %copy-done.6), kind=kOutput, calls=%fused_computation.13 | convolution fusion | flops 201327616 | bytes 5243136 | tf_op jit(solution)/shard_map/ks,kcb->scb/dot_general | solution.py:65
  108.6 0.7 copy.21
  109.4 4.2 %all-to-all-start.2 = ((bf16[8,1,128,128]{3,2,1,0:T(8,128)(2,1)}), bf16[8,1,128,128]{3,2,1,0:T(8,128)(2,1)S(1)}, u32[]{:S(2)}, u32[]{:S(2)}) async-start(bf16[8,1,128,128]{3,2,1,0:T(8,128)(2,1)} %copy.21), calls=%async_computation.2 | async-start | bytes 524288 | tf_op jit(solution)/shard_map/all_to_all | solution.py:68
  113.6 3.8 %copy_add_fusion = f32[4,128,1024]{1,2,0:T(8,128)} fusion(f32[4,128,1024]{1,2,0:T(8,128)} %copy.20, f32[4,128,1024]{1,0,2:T(4,128)} %reshape.34), kind=kLoop, calls=%fused_computation.20 | loop fusion | flops 524288 | bytes 6291456 | tf_op jit(solution)/shard_map/add | solution.py:50
  117.4 6.0 %all-to-all-done.2 = bf16[8,1,128,128]{3,2,1,0:T(8,128)(2,1)S(1)} async-done(((bf16[8,1,128,128]{3,2,1,0:T(8,128)(2,1)}), bf16[8,1,128,128]{3,2,1,0:T(8,128)(2,1)S(1)}, u32[]{:S(2)}, u32[]{:S(2)}) %all-to-all-start.2) | async-done | bytes 262176 | tf_op jit(solution)/shard_map/all_to_all | solution.py:68
  123.4 4.6 %all-to-all-start.1 = ((f32[4,128,1024]{1,2,0:T(8,128)}), f32[4,128,1024]{1,2,0:T(8,128)}, u32[]{:S(2)}, u32[]{:S(2)}) async-start(f32[4,128,1024]{1,2,0:T(8,128)} %copy_add_fusion), calls=%async_computation.1 | async-start | bytes 4194304 | tf_op jit(solution)/shard_map/all_to_all | solution.py:53
  128.0 2.5 %fusion.26 = f32[8,128,128]{2,1,0:T(8,128)} fusion(bf16[8,128,512]{2,1,0:T(8,128)(2,1)} %bitcast.82, bf16[128,512]{1,0:T(8,128)(2,1)S(1)} %copy-done.4), kind=kOutput, calls=%fused_computation.33 | convolution fusion | flops 134217728 | bytes 1703936 | tf_op jit(solution)/shard_map/iae,ce->iac/dot_general | solution.py:79
  130.4 2.1 copy.23
  132.5 2.1 fusion.22
  134.6 2.0 copy.36
  136.6 37.5 %all-to-all-done.1 = f32[4,128,1024]{1,2,0:T(8,128)} async-done(((f32[4,128,1024]{1,2,0:T(8,128)}), f32[4,128,1024]{1,2,0:T(8,128)}, u32[]{:S(2)}, u32[]{:S(2)}) %all-to-all-start.1) | async-done | bytes 2097184 | tf_op jit(solution)/shard_map/all_to_all | solution.py:53
  174.2 2.5 %reduce_sum.9 = bf16[128,1024]{0,1:T(8,128)(2,1)} reduce(f32[4,128,1024]{1,2,0:T(8,128)} %all-to-all-done.1, f32[]{:T(128)} %constant.2.clone.1), dimensions={0}, to_apply=%region_0.0 | reduce | flops 393216 | bytes 2359300 | tf_op jit(solution)/shard_map/reduce_sum | solution.py:53
  176.7 28.1 %all-reduce.2.cloned.1.call-done = f32[30,128,512]{2,1,0:T(8,128)} async-done(((f32[30,128,512]{2,1,0:T(8,128)}), f32[30,128,512]{2,1,0:T(8,128)}) %all-reduce.2.cloned.1.call-update) | async-done | bytes 7864336 | tf_op jit(solution)/shard_map/psum | solution.py:45
  204.8 6.3 %multiply_convert_fusion = bf16[30,128,512]{2,1,0:T(8,128)(2,1)} fusion(f32[30,128,512]{2,1,0:T(8,128)} %all-reduce.2.cloned.1.call-done), kind=kLoop, calls=%fused_computation.9 | loop fusion | flops 3932160 | bytes 11796480 | tf_op jit(solution)/shard_map/convert_element_type | solution.py:46
  (13 shorter events, 0.1 us)
Async XLA Ops:
  7.2 18.4 %copy-start = (bf16[64,128,128]{2,1,0:T(8,128)(2,1)S(1)}, bf16[64,128,128]{2,1,0:T(8,128)(2,1)}, u32[]{:S(2)}) copy-start(bf16[64,128,128]{2,1,0:T(8,128)(2,1)} %param.11) | copy-start | bytes 6291460
  7.2 53.3 %all-gather.2.cloned.1.call-start = ((), (), s32[]{:S(2)}) async-start(), calls=%async_computation.3 | async-start | bytes 1310720 | tf_op jit(solution)/shard_map/all_gather | solution.py:41
  7.9 15.2 %copy-start.8 = (f32[256,30]{0,1:T(8,128)S(1)}, f32[256,30]{0,1:T(8,128)}, u32[]{:S(2)}) copy-start(f32[256,30]{0,1:T(8,128)} %param.16) | copy-start | bytes 92164
  7.9 15.2 %copy-start.9 = (s32[64]{0:T(128)S(1)}, s32[64]{0:T(128)}, u32[]{:S(2)}) copy-start(s32[64]{0:T(128)} %param.14) | copy-start | bytes 772
  7.9 15.5 %copy-start.2 = (bf16[1024,128]{1,0:T(8,128)(2,1)S(1)}, bf16[1024,128]{1,0:T(8,128)(2,1)}, u32[]{:S(2)}) copy-start(bf16[1024,128]{1,0:T(8,128)(2,1)} %param.10) | copy-start | bytes 786436
  10.9 12.5 %all-to-all-start = ((bf16[8,1,128,128]{2,3,1,0:T(8,128)(2,1)}), bf16[8,1,128,128]{2,3,1,0:T(8,128)(2,1)S(1)}, u32[]{:S(2)}, u32[]{:S(2)}) async-start(bf16[8,1,128,128]{2,3,1,0:T(8,128)(2,1)} %bitcast.6), calls=%async_computation | async-start | bytes 524288 | tf_op jit(solution)/shard_map/all_to_all | solution.py:23
  16.1 188.7 %all-reduce.2.cloned.1.call-start = ((), (), s32[]{:S(2)}) async-start(), calls=%async_computation.4 | async-start | bytes 15728640 | tf_op jit(solution)/shard_map/psum | solution.py:45
  28.8 23.3 %copy-start.7 = (bf16[30,128,512]{2,1,0:T(8,128)(2,1)S(1)}, bf16[30,128,512]{2,1,0:T(8,128)(2,1)}, u32[]{:S(2)}) copy-start(bf16[30,128,512]{2,1,0:T(8,128)(2,1)} %param.17) | copy-start | bytes 11796484
  49.0 3.1 %copy-start.1 = (bf16[30,8,128,128]{3,1,2,0:T(8,128)(2,1)}, bf16[30,8,128,128]{3,1,2,0:T(8,128)(2,1)S(1)}, u32[]{:S(2)}) copy-start(bf16[30,8,128,128]{3,1,2,0:T(8,128)(2,1)S(1)} %convolution_convert_fusion) | copy-start | bytes 23592964
  60.5 8.9 %copy-start.3 = (bf16[1024,512]{1,0:T(8,128)(2,1)S(1)}, bf16[1024,512]{1,0:T(8,128)(2,1)}, u32[]{:S(2)}) copy-start(bf16[1024,512]{1,0:T(8,128)(2,1)} %all-gather.2.cloned.1.call-done) | copy-start | bytes 3145732
  102.7 2.1 copy-start.6
  109.4 14.0 %all-to-all-start.2 = ((bf16[8,1,128,128]{3,2,1,0:T(8,128)(2,1)}), bf16[8,1,128,128]{3,2,1,0:T(8,128)(2,1)S(1)}, u32[]{:S(2)}, u32[]{:S(2)}) async-start(bf16[8,1,128,128]{3,2,1,0:T(8,128)(2,1)} %copy.21), calls=%async_computation.2 | async-start | bytes 524288 | tf_op jit(solution)/shard_map/all_to_all | solution.py:68
  113.6 14.4 %copy-start.4 = (bf16[128,512]{1,0:T(8,128)(2,1)S(1)}, bf16[128,512]{1,0:T(8,128)(2,1)}, u32[]{:S(2)}) copy-start(bf16[128,512]{1,0:T(8,128)(2,1)} %param.18) | copy-start | bytes 393220
  117.4 15.1 %copy-start.5 = (s32[8,1]{0,1:T(1,128)S(1)}, s32[8,1]{0,1:T(1,128)}, u32[]{:S(2)}) copy-start(s32[8,1]{0,1:T(1,128)} %param.15) | copy-start | bytes 100
  123.4 50.8 %all-to-all-start.1 = ((f32[4,128,1024]{1,2,0:T(8,128)}), f32[4,128,1024]{1,2,0:T(8,128)}, u32[]{:S(2)}, u32[]{:S(2)}) async-start(f32[4,128,1024]{1,2,0:T(8,128)} %copy_add_fusion), calls=%async_computation.1 | async-start | bytes 4194304 | tf_op jit(solution)/shard_map/all_to_all | solution.py:53
Sparse Core Ops, SparseCore 0:
  9.6 32.8 all-gather.1
  78.9 125.8 all-reduce.1

commit v2 on v1

--- a/solution.py
+++ b/solution.py
@@ -35,13 +35,16 @@
     )
     block_coef = jnp.dot(rel_select, coef, precision=exact_products)
     summed = jnp.einsum(
-        "ki,kb,kca->bica", row_select, block_coef, message, precision=exact_products
+        "ki,kb,kca->bica", row_select, block_coef, message, precision=lax.Precision.HIGH
     ).astype(jnp.bfloat16)
     scale_factor = 1.0 / math.sqrt(partitions * node_count)
     grad_full = lax.all_gather(cotangent, "feat", axis=1, tiled=True).reshape(
         owned_blocks, blk_size, full_width
     )
     basis_part = jnp.einsum("bica,iae->bce", summed, grad_full, preferred_element_type=jnp.float32)
+    basis_part, summed, grad_full, bases = lax.optimization_barrier(
+        (basis_part, summed, grad_full, bases)
+    )
     basis_total = lax.psum(basis_part, "node")
     basis_grad = (basis_total * scale_factor).astype(jnp.bfloat16)
     combined = jnp.einsum("bica,bco->oia", summed, bases, preferred_element_type=jnp.float32)

time: 219 us -> 189 us (0.86); the launches traced: 218 us -> 186 us
  waiting for transfers between devices: 72.3 us -> 47.2 us
  matrix products: 84.5 us -> 79.7 us
    psum x1, waiting for transfers between devices: 28.1 us -> 1.71 us  [body(): basis_total = lax.psum(basis_part, 'node')]
    dot_general x1, matrix products: 20.2 us -> 11.3 us  [body(): jnp.einsum('ki,kb,kca->bica', row_select, block_coef, message, precision=...]
    all_to_all x1, waiting for transfers between devices: 5.97 us -> 0.01 us  [body(): lax.all_to_all(leaving.astype(jnp.bfloat16), 'node', split_axis=0, concat...]
    dot_general x1, matrix products: 5.57 us -> 9.01 us  [body(): jnp.einsum('bica,bco->oia', summed, bases, preferred_element_type=jnp.flo...]
    all_gather x1, waiting for transfers between devices: 0.01 us -> 2.94 us  [body(): lax.all_gather(cotangent, 'feat', axis=1, tiled=True)]
    reshape x1 -> x0, local copies, waits for them, and re-layouts: 2.91 us -> none  [body(): combined = combined.reshape(feat_parts, out_cols, node_count) + jnp.einsu...]
    dot_general x1, matrix products: 9.32 us -> 6.5 us  [body(): jnp.einsum('iae,bce->bica', grad_full, bases, preferred_element_type=jnp....]
    dot_general x1, matrix products: 23.9 us -> 26.6 us  [body(): jnp.einsum('ki,kb,bica->kca', row_select, block_coef, grad_summed, precis...]
  transfers between devices with their start and end apart: 5 -> 5, of which waited for: 3 -> 4; matrix products, arithmetic and copies ran while one was open for 41% -> 51% of each run, Pallas kernels for 0% -> 0%
where the time goes in v2:
time: 189 us; the launch traced here: 186 us
  matrix products  79.7 us (42%)
  waiting for transfers between devices  47.2 us (25%)
  local copies, waits for them, and re-layouts  16.6 us (9%)
  other arithmetic  14.4 us (8%)
  between operations  14.3 us (8%)
  starting transfers between devices  13.5 us (7%)
    all_to_all x1, waiting for transfers between devices, body(): lax.all_to_all(combined, 'feat', split_axis=0, concat_axis=0, tiled=True)  40.2 us
    dot_general x1, matrix products, body(): jnp.einsum('ki,kb,bica->kca', row_select, block_coef, grad_summed, precis...  26.6 us
    dot_general x1, matrix products, body(): jnp.einsum('ki,kb,kca->bica', row_select, block_coef, message, precision=...  11.3 us
    dot_general x1, matrix products, body(): jnp.einsum('bica,bco->oia', summed, bases, preferred_element_type=jnp.flo...  9.01 us
    dot_general x1, matrix products, body(): jnp.einsum('bica,iae->bce', summed, grad_full, preferred_element_type=jnp...  8.76 us
    dot_general x1, matrix products, body(): jnp.einsum('iae,bce->bica', grad_full, bases, preferred_element_type=jnp....  6.5 us
    convert_element_type x1, other arithmetic, body(): basis_grad = (basis_total * scale_factor).astype(jnp.bfloat16)  6.35 us
    all_to_all x1, starting transfers between devices, body(): lax.all_to_all(outgoing, 'node', split_axis=0, concat_axis=0, tiled=True)  5.17 us
  transfers between devices with their start and end apart: 5, of which 4 were waited for; matrix products, arithmetic and copies ran while one was open for 51% of the time, Pallas kernels for 0%

profile of v2, /device:TPU:0, one launch (start us, length us, event | category | flops | bytes accessed | tf_op | source)
XLA Modules:
  0.0 185.7 jit_solution(12420705377445171090)
XLA Ops:
  7.2 0.0 copy-start
  7.2 0.0 copy-start.1
  7.2 0.0 all-gather.2.cloned.1.call-start
  7.2 0.7 all-gather.2.cloned.1.call-update
  7.9 0.7 fusion.44
  8.6 2.2 %gather_fusion = bf16[8,128,128]{1,2,0:T(8,128)(2,1)} fusion(bf16[8,128,128]{1,2,0:T(8,128)(2,1)} %bitcast.76, s32[1024]{0:T(1024)S(1)} %pad_clamp_fusion.1), kind=kCustom, calls=%fused_computation | custom fusion | bytes 524320 | tf_op jit(solution)/shard_map/gather | solution.py:22
  10.8 5.2 %all-to-all-start = ((bf16[8,1,128,128]{2,3,1,0:T(8,128)(2,1)}), bf16[8,1,128,128]{2,3,1,0:T(8,128)(2,1)S(1)}, u32[]{:S(2)}, u32[]{:S(2)}) async-start(bf16[8,1,128,128]{2,3,1,0:T(8,128)(2,1)} %bitcast.6), calls=%async_computation | async-start | bytes 524288 | tf_op jit(solution)/shard_map/all_to_all | solution.py:23
  16.0 0.0 all-reduce.2.cloned.1.call-start
  16.0 0.7 fusion.40
  16.7 2.9 %fusion.46 = f32[512,1024]{1,0:T(8,128)} fusion(bf16[128,512]{1,0:T(8,128)(2,1)} %param.18, bf16[1024,128]{1,0:T(8,128)(2,1)} %param.10), kind=kOutput, calls=%fused_computation.56 | convolution fusion | flops 134217728 | bytes 2490368 | tf_op jit(solution)/shard_map/nc,co->on/dot_general | solution.py:53
  19.6 1.0 fusion.33
  20.6 0.7 compare_select_fusion
  21.3 1.6 all-to-all-done
  22.9 0.0 copy-done.1
  23.0 2.1 %gather_fusion.1 = bf16[64,128,128]{1,2,0:T(8,128)(2,1)} fusion(bf16[16,128,128]{1,2,0:T(8,128)(2,1)S(1)} %pad_maximum_fusion, s32[1024]{0:T(1024)S(1)} %pad_clamp_fusion), kind=kCustom, calls=%fused_computation.1 | custom fusion | bytes 4194560 | tf_op jit(solution)/shard_map/gather | solution.py:28
  25.1 0.0 copy-done
  25.1 3.2 %fusion.45 = f32[64,128,128]{2,1,0:T(8,128)S(1)} fusion(bf16[64,128,128]{1,2,0:T(8,128)(2,1)} %gather_fusion.1, bf16[64,128,128]{2,1,0:T(8,128)(2,1)S(1)} %copy-done), kind=kOutput, calls=%fused_computation.55 | convolution fusion | flops 268435456 | bytes 8388608 | tf_op jit(solution)/shard_map/kab,kcb->kca/dot_general | solution.py:29
  28.3 11.3 %convolution_convert_fusion = bf16[30,8,128,128]{3,1,2,0:T(8,128)(2,1)} fusion(f32[64,128,128]{2,1,0:T(8,128)S(1)} %fusion.45, f32[64,8]{0,1:T(8,128)S(1)} %fusion.40, f32[64,30]{0,1:T(8,128)S(1)} %fusion.33), kind=kOutput, calls=%fused_computation.10 | convolution fusion | flops 1513896960 | bytes 12068352 | tf_op jit(solution)/shard_map/ki,kb,kca->bica/dot_general | solution.py:37
  39.6 2.9 %all-gather.2.cloned.1.call-done = bf16[1024,512]{1,0:T(8,128)(2,1)} async-done(((bf16[1024,128]{1,0:T(8,128)(2,1)}), bf16[1024,512]{1,0:T(8,128)(2,1)}) %all-gather.2.cloned.1.call-update) | async-done | bytes 1048592 | tf_op jit(solution)/shard_map/all_gather | solution.py:41
  42.5 8.8 %fusion.12 = f32[30,128,512]{2,1,0:T(8,128)} fusion(bf16[8,128,512,1]{2,1,0,3:T(8,128)(2,1)} %bitcast.79, bf16[30,8,128,128]{3,1,2,0:T(8,128)(2,1)} %convolution_convert_fusion), kind=kOutput, calls=%fused_computation.18 | convolution fusion | flops 4026531840 | bytes 16777216 | tf_op jit(solution)/shard_map/bica,iae->bce/dot_general | solution.py:44
  51.3 0.0 copy-start.2
  51.3 0.0 all-reduce.2.cloned.1.call-update
  51.3 1.2 copy-done.2
  52.5 6.5 %convolution_bitcast_fusion = f32[30,8,128,128]{3,2,1,0:T(8,128)S(1)} fusion(bf16[30,128,512]{2,1,0:T(8,128)(2,1)} %param.17, bf16[8,128,512]{2,1,0:T(8,128)(2,1)S(1)} %bitcast.81), kind=kOutput, calls=%fused_computation.4 | convolution fusion | flops 4026531840 | bytes 20709376 | tf_op jit(solution)/shard_map/iae,bce->bica/dot_general | solution.py:58
  59.0 26.6 %bitcast_convert_fusion = bf16[64,128,128]{2,0,1:T(8,128)(2,1)S(1)} fusion(f32[30,8,128,128]{3,2,1,0:T(8,128)S(1)} %convolution_bitcast_fusion, f32[64,30,8,1]{0,2,1,3:T(8,128)S(1)} %multiply_bitcast_fusion.1), kind=kOutput, calls=%fused_computation.11 | convolution fusion | flops 3020947456 | bytes 17887232 | tf_op jit(solution)/shard_map/ki,kb,bica->kca/dot_general | solution.py:59
  85.6 0.0 copy-start.5
  85.6 2.0 %fusion.17 = f32[64,128,128]{2,1,0:T(8,128)S(1)} fusion(bf16[64,128,128]{2,1,0:T(8,128)(2,1)S(1)} %copy-done, bf16[64,128,128]{2,0,1:T(8,128)(2,1)S(1)} %bitcast_convert_fusion), kind=kOutput, calls=%fused_computation.19 | convolution fusion | flops 268435456 | bytes 8388608 | tf_op jit(solution)/shard_map/kab,kca->kcb/dot_general | solution.py:62
  87.6 0.0 copy-done.5
  87.6 3.8 %fusion.7 = f32[16,128,128]{2,0,1:T(8,128)S(1)} fusion(f32[64,128,128]{2,1,0:T(8,128)S(1)} %fusion.17, s32[64]{0:T(128)S(1)} %copy-done.5), kind=kOutput, calls=%fused_computation.13 | convolution fusion | flops 201327616 | bytes 5243136 | tf_op jit(solution)/shard_map/ks,kcb->scb/dot_general | solution.py:68
  91.5 0.7 copy.33
  92.2 3.4 %all-to-all-start.2 = ((bf16[8,1,128,128]{3,2,1,0:T(8,128)(2,1)}), bf16[8,1,128,128]{3,2,1,0:T(8,128)(2,1)S(1)}, u32[]{:S(2)}, u32[]{:S(2)}) async-start(bf16[8,1,128,128]{3,2,1,0:T(8,128)(2,1)} %copy.33), calls=%async_computation.2 | async-start | bytes 524288 | tf_op jit(solution)/shard_map/all_to_all | solution.py:71
  95.6 9.0 %fusion.19 = f32[512,8,128]{2,0,1:T(8,128)S(1)} fusion(bf16[30,8,128,128]{3,1,2,0:T(8,128)(2,1)} %convolution_convert_fusion, bf16[30,128,512]{2,1,0:T(8,128)(2,1)} %param.17), kind=kOutput, calls=%fused_computation.21 | convolution fusion | flops 4026531840 | bytes 13893632 | tf_op jit(solution)/shard_map/bica,bco->oia/dot_general | solution.py:50
  104.7 2.5 %copy.29 = f32[512,8,128]{2,1,0:T(8,128)} copy(f32[512,8,128]{2,0,1:T(8,128)S(1)} %fusion.19) | data formatting | bytes 4194304 | tf_op jit(solution)/shard_map/bica,bco->oia/dot_general | solution.py:50
  107.2 2.7 %reshape.35 = f32[4,128,1024]{2,1,0:T(8,128)} reshape(f32[512,8,128]{2,1,0:T(8,128)} %copy.29) | data formatting | bytes 4194304 | tf_op jit(solution)/shard_map/reshape | solution.py:53
  109.9 4.2 %add.23 = f32[4,128,1024]{2,1,0:T(8,128)} add(f32[4,128,1024]{2,1,0:T(8,128)} %reshape.35, f32[4,128,1024]{2,1,0:T(8,128)} %bitcast.75) | non-fusion elementwise | flops 524288 | bytes 6291456 | tf_op jit(solution)/shard_map/add | solution.py:53
  114.1 0.0 all-to-all-done.2
  114.1 4.8 %all-to-all-start.1 = ((f32[4,128,1024]{2,1,0:T(8,128)}), f32[4,128,1024]{2,1,0:T(8,128)}, u32[]{:S(2)}, u32[]{:S(2)}) async-start(f32[4,128,1024]{2,1,0:T(8,128)} %add.23), calls=%async_computation.1 | async-start | bytes 4194304 | tf_op jit(solution)/shard_map/all_to_all | solution.py:56
  119.0 0.0 copy-done.3
  119.0 2.6 %fusion.30 = f32[8,128,128]{2,1,0:T(8,128)} fusion(bf16[8,128,512]{2,1,0:T(8,128)(2,1)} %bitcast.80, bf16[128,512]{1,0:T(8,128)(2,1)S(1)} %copy-done.3), kind=kOutput, calls=%fused_computation.34 | convolution fusion | flops 134217728 | bytes 1703936 | tf_op jit(solution)/shard_map/iae,ce->iac/dot_general | solution.py:82
  121.5 2.1 %copy.35 = f32[8,128,128]{1,0,2:T(8,128)} copy(f32[8,128,128]{2,1,0:T(8,128)} %fusion.30) | data formatting | bytes 1048576 | tf_op jit(solution)/shard_map/iae,ce->iac/dot_general | solution.py:82
  123.6 0.0 copy-done.4
  123.6 2.1 %fusion.25 = f32[8,128,128]{1,0,2:T(8,128)} fusion(f32[8,128,128]{1,0,2:T(8,128)} %copy.35, f32[16,128,128]{2,0,1:T(8,128)S(1)} %fusion.7, bf16[8,1,128,128]{3,2,1,0:T(8,128)(2,1)S(1)} %all-to-all-done.2, s32[8]{0:T(128)S(1)} %bitcast.84), kind=kOutput, calls=%fused_computation.24 | convolution fusion | flops 2359360 | bytes 1835040 | tf_op jit(solution)/shard_map/ti,tcb->icb/dot_general | solution.py:80
  125.7 2.0 %copy.49 = f32[8,128,128]{2,1,0:T(8,128)} copy(f32[8,128,128]{1,0,2:T(8,128)} %fusion.25) | data formatting | bytes 1048576
  127.7 40.2 %all-to-all-done.1 = f32[4,128,1024]{2,1,0:T(8,128)} async-done(((f32[4,128,1024]{2,1,0:T(8,128)}), f32[4,128,1024]{2,1,0:T(8,128)}, u32[]{:S(2)}, u32[]{:S(2)}) %all-to-all-start.1) | async-done | bytes 2097184 | tf_op jit(solution)/shard_map/all_to_all | solution.py:56
  167.9 1.8 reduce_sum.9
  169.7 0.8 copy.36
  170.6 1.7 all-reduce.2.cloned.1.call-done
  172.3 6.3 %multiply_convert_fusion = bf16[30,128,512]{2,1,0:T(8,128)(2,1)} fusion(f32[30,128,512]{2,1,0:T(8,128)} %all-reduce.2.cloned.1.call-done), kind=kLoop, calls=%fused_computation.9 | loop fusion | flops 3932160 | bytes 11796480 | tf_op jit(solution)/shard_map/convert_element_type | solution.py:49
  (7 shorter events, 0.1 us)
Async XLA Ops:
  7.2 18.0 %copy-start = (bf16[64,128,128]{2,1,0:T(8,128)(2,1)S(1)}, bf16[64,128,128]{2,1,0:T(8,128)(2,1)}, u32[]{:S(2)}) copy-start(bf16[64,128,128]{2,1,0:T(8,128)(2,1)} %param.11) | copy-start | bytes 6291460
  7.2 15.8 %copy-start.1 = (bf16[1024,128]{1,0:T(8,128)(2,1)S(1)}, bf16[1024,128]{1,0:T(8,128)(2,1)}, u32[]{:S(2)}) copy-start(bf16[1024,128]{1,0:T(8,128)(2,1)} %param.10) | copy-start | bytes 786436
  7.2 35.3 %all-gather.2.cloned.1.call-start = ((), (), s32[]{:S(2)}) async-start(), calls=%async_computation.3 | async-start | bytes 1310720 | tf_op jit(solution)/shard_map/all_gather | solution.py:41
  10.8 12.1 %all-to-all-start = ((bf16[8,1,128,128]{2,3,1,0:T(8,128)(2,1)}), bf16[8,1,128,128]{2,3,1,0:T(8,128)(2,1)S(1)}, u32[]{:S(2)}, u32[]{:S(2)}) async-start(bf16[8,1,128,128]{2,3,1,0:T(8,128)(2,1)} %bitcast.6), calls=%async_computation | async-start | bytes 524288 | tf_op jit(solution)/shard_map/all_to_all | solution.py:23
  16.0 156.3 %all-reduce.2.cloned.1.call-start = ((), (), s32[]{:S(2)}) async-start(), calls=%async_computation.4 | async-start | bytes 15728640 | tf_op jit(solution)/shard_map/psum | solution.py:48
  51.3 1.2 copy-start.2
  85.6 2.1 %copy-start.5 = (s32[64]{0:T(128)S(1)}, s32[64]{0:T(128)}, u32[]{:S(2)}) copy-start(s32[64]{0:T(128)} %param.13) | copy-start | bytes 772
  92.2 21.9 %all-to-all-start.2 = ((bf16[8,1,128,128]{3,2,1,0:T(8,128)(2,1)}), bf16[8,1,128,128]{3,2,1,0:T(8,128)(2,1)S(1)}, u32[]{:S(2)}, u32[]{:S(2)}) async-start(bf16[8,1,128,128]{3,2,1,0:T(8,128)(2,1)} %copy.33), calls=%async_computation.2 | async-start | bytes 524288 | tf_op jit(solution)/shard_map/all_to_all | solution.py:71
  109.9 9.0 %copy-start.3 = (bf16[128,512]{1,0:T(8,128)(2,1)S(1)}, bf16[128,512]{1,0:T(8,128)(2,1)}, u32[]{:S(2)}) copy-start(bf16[128,512]{1,0:T(8,128)(2,1)} %param.18) | copy-start | bytes 393220
  114.1 9.5 %copy-start.4 = (s32[8,1]{0,1:T(1,128)S(1)}, s32[8,1]{0,1:T(1,128)}, u32[]{:S(2)}) copy-start(s32[8,1]{0,1:T(1,128)} %param.15) | copy-start | bytes 100
  114.1 53.8 %all-to-all-start.1 = ((f32[4,128,1024]{2,1,0:T(8,128)}), f32[4,128,1024]{2,1,0:T(8,128)}, u32[]{:S(2)}, u32[]{:S(2)}) async-start(f32[4,128,1024]{2,1,0:T(8,128)} %add.23), calls=%async_computation.1 | async-start | bytes 4194304 | tf_op jit(solution)/shard_map/all_to_all | solution.py:56
Sparse Core Ops, SparseCore 0:
  9.6 32.8 all-gather.1
  51.4 120.8 all-reduce.1

commit v3 on v2

--- a/solution.py
+++ b/solution.py
@@ -33,7 +33,7 @@
     rel_select = (block_rel[:, None] == jnp.arange(relations, dtype=jnp.int32)[None, :]).astype(
         jnp.float32
     )
-    block_coef = jnp.dot(rel_select, coef, precision=exact_products)
+    block_coef = coef[block_rel]
     summed = jnp.einsum(
         "ki,kb,kca->bica", row_select, block_coef, message, precision=lax.Precision.HIGH
     ).astype(jnp.bfloat16)
@@ -57,7 +57,7 @@
     layer_out = jnp.transpose(layer_cols).astype(jnp.bfloat16)
     grad_summed = jnp.einsum("iae,bce->bica", grad_full, bases, preferred_element_type=jnp.float32)
     grad_message = jnp.einsum(
-        "ki,kb,bica->kca", row_select, block_coef, grad_summed, precision=exact_products
+        "ki,kb,bica->kca", row_select, block_coef, grad_summed, precision=lax.Precision.HIGH
     ).astype(jnp.bfloat16)
     grad_source = jnp.einsum(
         "kab,kca->kcb", tiles, grad_message, preferred_element_type=jnp.float32
@@ -65,7 +65,9 @@
     col_select = (
         block_col[:, None] == jnp.arange(slot_count_total, dtype=jnp.int32)[None, :]
     ).astype(jnp.float32)
-    slot_grad = jnp.einsum("ks,kcb->scb", col_select, grad_source, precision=exact_products)
+    slot_grad = jnp.zeros((slot_count_total,) + grad_source.shape[1:], jnp.float32).at[block_col].add(
+        grad_source
+    )
     leaving = slot_grad[owned_blocks:].reshape(partitions, per_peer, col_width, blk_size)
     returned = (
         lax.all_to_all(
@@ -77,7 +79,9 @@
     send_select = (
         send_list.reshape(-1)[:, None] == jnp.arange(owned_blocks, dtype=jnp.int32)[None, :]
     ).astype(jnp.float32)
-    arrived = jnp.einsum("ti,tcb->icb", send_select, returned, precision=exact_products)
+    arrived = jnp.zeros((owned_blocks,) + returned.shape[1:], jnp.float32).at[send_list.reshape(-1)].add(
+        returned
+    )
     own_grad = jnp.transpose(slot_grad[:owned_blocks] + arrived, (0, 2, 1))
     self_loop_gradient = jnp.einsum(
         "iae,ce->iac", grad_full, self_weight, preferred_element_type=jnp.float32

time: 189 us -> 189 us (level); the launches traced: 186 us -> 188 us
  other arithmetic: 14.4 us -> 27.1 us
  matrix products: 79.7 us -> 72.8 us
    scatter-add x0 -> x2, other arithmetic: none -> 11.5 us  [the longest x1 8.79 us: body(): jnp.zeros((slot_count_total,) + grad_source.shape[1:], jnp.float32)]
    dot_general x3 -> x0, matrix products: 6.93 us -> none  [the longest x1 3.81 us: body(): jnp.einsum('ks,kcb->scb', col_select, grad_source, precision=exact_products)]
    dot_general x1, matrix products: 2.04 us -> 5.63 us  [body(): jnp.einsum('kab,kca->kcb', tiles, grad_message, preferred_element_type=jn...]
    dot_general x1, matrix products: 26.6 us -> 23.1 us  [body(): jnp.einsum('ki,kb,bica->kca', row_select, block_coef, grad_summed, precis...]
    unnamed x14 -> x8, local copies, waits for them, and re-layouts: 4.11 us -> 1.73 us
    dot_general x1 -> x0, local copies, waits for them, and re-layouts: 2.06 us -> none  [body(): jnp.einsum('iae,ce->iac', grad_full, self_weight, preferred_element_type=...]
  transfers between devices with their start and end apart: 5 -> 5, of which waited for: 4 -> 3; matrix products, arithmetic and copies ran while one was open for 51% -> 53% of each run, Pallas kernels for 0% -> 0%
where the time goes in v3:
time: 189 us; the launch traced here: 188 us
  matrix products  72.8 us (39%)
  waiting for transfers between devices  45.7 us (24%)
  other arithmetic  27.1 us (14%)
  local copies, waits for them, and re-layouts  14.9 us (8%)
  between operations  14.1 us (7%)
  starting transfers between devices  13.3 us (7%)
    all_to_all x1, waiting for transfers between devices, body(): lax.all_to_all(combined, 'feat', split_axis=0, concat_axis=0, tiled=True)  41.8 us
    dot_general x1, matrix products, body(): jnp.einsum('ki,kb,bica->kca', row_select, block_coef, grad_summed, precis...  23.1 us
    dot_general x1, matrix products, body(): jnp.einsum('ki,kb,kca->bica', row_select, block_coef, message, precision=...  11.2 us
    dot_general x1, matrix products, body(): jnp.einsum('bica,iae->bce', summed, grad_full, preferred_element_type=jnp...  8.79 us
    scatter-add x1, other arithmetic, body(): jnp.zeros((slot_count_total,) + grad_source.shape[1:], jnp.float32)  8.79 us
    dot_general x1, matrix products, body(): jnp.einsum('bica,bco->oia', summed, bases, preferred_element_type=jnp.flo...  8.75 us
    dot_general x1, matrix products, body(): jnp.einsum('iae,bce->bica', grad_full, bases, preferred_element_type=jnp....  6.8 us
    convert_element_type x1, other arithmetic, body(): basis_grad = (basis_total * scale_factor).astype(jnp.bfloat16)  6.35 us
  transfers between devices with their start and end apart: 5, of which 3 were waited for; matrix products, arithmetic and copies ran while one was open for 53% of the time, Pallas kernels for 0%

profile of v3, /device:TPU:0, one launch (start us, length us, event | category | flops | bytes accessed | tf_op | source)
XLA Modules:
  0.0 187.9 jit_solution(15552285900118686268)
XLA Ops:
  7.2 0.0 copy-start
  7.2 0.0 copy-start.1
  7.2 0.0 all-gather.2.cloned.1.call-start
  7.2 0.7 all-gather.2.cloned.1.call-update
  7.9 0.7 fusion.29
  8.6 2.2 %gather_fusion.1 = bf16[8,128,128]{1,2,0:T(8,128)(2,1)} fusion(bf16[8,128,128]{1,2,0:T(8,128)(2,1)} %bitcast.68, s32[1024]{0:T(1024)S(1)} %pad_clamp_fusion.1), kind=kCustom, calls=%fused_computation.1 | custom fusion | bytes 524320 | tf_op jit(solution)/shard_map/gather | solution.py:22
  10.8 5.2 %all-to-all-start = ((bf16[8,1,128,128]{2,3,1,0:T(8,128)(2,1)}), bf16[8,1,128,128]{2,3,1,0:T(8,128)(2,1)S(1)}, u32[]{:S(2)}, u32[]{:S(2)}) async-start(bf16[8,1,128,128]{2,3,1,0:T(8,128)(2,1)} %bitcast.6), calls=%async_computation | async-start | bytes 524288 | tf_op jit(solution)/shard_map/all_to_all | solution.py:23
  16.0 0.0 all-reduce.2.cloned.1.call-start
  16.0 0.7 compare_select_fusion
  16.7 0.7 fusion.28
  17.4 2.8 %fusion.31 = f32[512,1024]{1,0:T(8,128)} fusion(bf16[128,512]{1,0:T(8,128)(2,1)} %param.18, bf16[1024,128]{1,0:T(8,128)(2,1)} %param.10), kind=kOutput, calls=%fused_computation.46 | convolution fusion | flops 134217728 | bytes 2490368 | tf_op jit(solution)/shard_map/nc,co->on/dot_general | solution.py:53
  20.2 0.7 compare_select_fusion.2
  20.9 0.9 copy.25
  21.8 0.6 gather_fusion
  22.4 0.1 copy.26
  22.4 0.7 multiply_bitcast_fusion.1
  23.1 0.0 all-to-all-done
  23.1 0.0 copy-done.1
  23.2 2.1 %gather_fusion.2 = bf16[64,128,128]{1,2,0:T(8,128)(2,1)} fusion(bf16[16,128,128]{1,2,0:T(8,128)(2,1)S(1)} %pad_maximum_fusion, s32[1024]{0:T(1024)S(1)} %pad_clamp_fusion), kind=kCustom, calls=%fused_computation.2 | custom fusion | bytes 4194560 | tf_op jit(solution)/shard_map/gather | solution.py:28
  25.3 0.0 copy-done
  25.3 3.2 %fusion.30 = f32[64,128,128]{2,1,0:T(8,128)S(1)} fusion(bf16[64,128,128]{1,2,0:T(8,128)(2,1)} %gather_fusion.2, bf16[64,128,128]{2,1,0:T(8,128)(2,1)S(1)} %copy-done), kind=kOutput, calls=%fused_computation.45 | convolution fusion | flops 268435456 | bytes 8388608 | tf_op jit(solution)/shard_map/kab,kcb->kca/dot_general | solution.py:29
  28.5 11.2 %convolution_convert_fusion = bf16[30,8,128,128]{3,1,2,0:T(8,128)(2,1)} fusion(f32[64,128,128]{2,1,0:T(8,128)S(1)} %fusion.30, f32[64,8]{0,1:T(8,128)S(1)} %fusion.28, f32[64,30]{0,1:T(8,128)S(1)} %copy.26), kind=kOutput, calls=%fused_computation.13 | convolution fusion | flops 1513896960 | bytes 12068352 | tf_op jit(solution)/shard_map/ki,kb,kca->bica/dot_general | solution.py:37
  39.7 2.8 %all-gather.2.cloned.1.call-done = bf16[1024,512]{1,0:T(8,128)(2,1)} async-done(((bf16[1024,128]{1,0:T(8,128)(2,1)}), bf16[1024,512]{1,0:T(8,128)(2,1)}) %all-gather.2.cloned.1.call-update) | async-done | bytes 1048592 | tf_op jit(solution)/shard_map/all_gather | solution.py:41
  42.5 8.8 %fusion.10 = f32[30,128,512]{2,1,0:T(8,128)} fusion(bf16[8,128,512,1]{2,1,0,3:T(8,128)(2,1)} %bitcast.71, bf16[30,8,128,128]{3,1,2,0:T(8,128)(2,1)} %convolution_convert_fusion), kind=kOutput, calls=%fused_computation.19 | convolution fusion | flops 4026531840 | bytes 16777216 | tf_op jit(solution)/shard_map/bica,iae->bce/dot_general | solution.py:44
  51.3 0.0 all-reduce.2.cloned.1.call-update
  51.3 6.8 %convolution_bitcast_fusion = f32[30,8,128,128]{3,2,1,0:T(8,128)S(1)} fusion(bf16[30,128,512]{2,1,0:T(8,128)(2,1)} %param.17, bf16[8,128,512]{2,1,0:T(8,128)(2,1)} %bitcast.72), kind=kOutput, calls=%fused_computation.7 | convolution fusion | flops 4026531840 | bytes 20709376 | tf_op jit(solution)/shard_map/iae,bce->bica/dot_general | solution.py:58
  58.1 23.1 %bitcast_convert_fusion = bf16[64,128,128]{2,0,1:T(8,128)(2,1)} fusion(f32[30,8,128,128]{3,2,1,0:T(8,128)S(1)} %convolution_bitcast_fusion, f32[64,30,8,1]{0,2,1,3:T(8,128)} %multiply_bitcast_fusion.1), kind=kOutput, calls=%fused_computation.14 | convolution fusion | flops 1510998016 | bytes 17887232 | tf_op jit(solution)/shard_map/ki,kb,bica->kca/dot_general | solution.py:59
  81.2 5.6 %fusion.15 = f32[64,128,128]{2,1,0:T(8,128)} fusion(bf16[64,128,128]{2,1,0:T(8,128)(2,1)S(1)} %copy-done, bf16[64,128,128]{2,0,1:T(8,128)(2,1)} %bitcast_convert_fusion), kind=kOutput, calls=%fused_computation.20 | convolution fusion | flops 268435456 | bytes 8388608 | tf_op jit(solution)/shard_map/kab,kca->kcb/dot_general | solution.py:62
  86.8 0.1 broadcast_in_dim.20
  86.9 8.8 %scatter_fusion = f32[16,128,128]{2,1,0:T(8,128)S(1)} fusion(f32[16,128,128]{2,1,0:T(8,128)S(1)} %broadcast_in_dim.20, s32[64]{0:T(128)S(1)} %compare_select_fusion, f32[64,128,128]{2,1,0:T(8,128)} %fusion.15), kind=kCustom, calls=%fused_computation.3 | custom fusion | flops 1048576 | bytes 12583168 | tf_op jit(solution)/shard_map/scatter-add | solution.py:68
  95.7 0.7 fusion.23
  96.5 3.4 %all-to-all-start.2 = ((bf16[8,1,128,128]{3,2,1,0:T(8,128)(2,1)}), bf16[8,1,128,128]{3,2,1,0:T(8,128)(2,1)S(1)}, u32[]{:S(2)}, u32[]{:S(2)}) async-start(bf16[8,1,128,128]{3,2,1,0:T(8,128)(2,1)} %fusion.23), calls=%async_computation.2 | async-start | bytes 524288 | tf_op jit(solution)/shard_map/all_to_all | solution.py:73
  99.9 8.8 %fusion.17 = f32[512,8,128]{2,0,1:T(8,128)S(1)} fusion(bf16[30,8,128,128]{3,1,2,0:T(8,128)(2,1)} %convolution_convert_fusion, bf16[30,128,512]{2,1,0:T(8,128)(2,1)} %param.17), kind=kOutput, calls=%fused_computation.22 | convolution fusion | flops 4026531840 | bytes 13893632 | tf_op jit(solution)/shard_map/bica,bco->oia/dot_general | solution.py:50
  108.7 2.5 %copy.32 = f32[512,8,128]{2,1,0:T(8,128)} copy(f32[512,8,128]{2,0,1:T(8,128)S(1)} %fusion.17) | data formatting | bytes 4194304 | tf_op jit(solution)/shard_map/bica,bco->oia/dot_general | solution.py:50
  111.2 2.7 %reshape.37 = f32[4,128,1024]{2,1,0:T(8,128)} reshape(f32[512,8,128]{2,1,0:T(8,128)} %copy.32) | data formatting | bytes 4194304 | tf_op jit(solution)/shard_map/reshape | solution.py:53
  113.9 4.1 %add.33 = f32[4,128,1024]{2,1,0:T(8,128)} add(f32[4,128,1024]{2,1,0:T(8,128)} %reshape.37, f32[4,128,1024]{2,1,0:T(8,128)} %bitcast.67) | non-fusion elementwise | flops 524288 | bytes 6291456 | tf_op jit(solution)/shard_map/add | solution.py:53
  118.0 0.0 all-to-all-done.2
  118.0 4.7 %all-to-all-start.1 = ((f32[4,128,1024]{2,1,0:T(8,128)}), f32[4,128,1024]{2,1,0:T(8,128)}, u32[]{:S(2)}, u32[]{:S(2)}) async-start(f32[4,128,1024]{2,1,0:T(8,128)} %add.33), calls=%async_computation.1 | async-start | bytes 4194304 | tf_op jit(solution)/shard_map/all_to_all | solution.py:56
  122.7 0.8 slice.15
  123.5 2.7 %scatter_fusion.1 = f32[8,128,128]{2,1,0:T(8,128)} fusion(f32[8,128,128]{2,1,0:T(8,128)} %slice.15, s32[8]{0:T(128)S(1)} %fusion.29, f32[8,128,128]{2,1,0:T(8,128)S(1)} %bitcast_convert_fusion.1), kind=kCustom, calls=%fused_computation.4 | custom fusion | flops 131072 | bytes 1572896 | tf_op jit(solution)/shard_map/scatter-add | solution.py:82
  126.2 1.2 copy.36
  127.5 0.0 copy-done.2
  127.5 2.5 %convolution_add_fusion = f32[8,128,128]{2,1,0:T(8,128)} fusion(bf16[8,128,512]{2,1,0:T(8,128)(2,1)} %bitcast.73, f32[8,128,128]{1,2,0:T(8,128)S(1)} %copy.36, bf16[128,512]{1,0:T(8,128)(2,1)S(1)} %copy-done.2), kind=kOutput, calls=%fused_computation.23 | convolution fusion | flops 134348800 | bytes 2228224 | tf_op jit(solution)/shard_map/iae,ce->iac/dot_general | solution.py:86
  129.9 41.8 %all-to-all-done.1 = f32[4,128,1024]{2,1,0:T(8,128)} async-done(((f32[4,128,1024]{2,1,0:T(8,128)}), f32[4,128,1024]{2,1,0:T(8,128)}, u32[]{:S(2)}, u32[]{:S(2)}) %all-to-all-start.1) | async-done | bytes 2097184 | tf_op jit(solution)/shard_map/all_to_all | solution.py:56
  171.7 1.8 reduce_sum.9
  173.6 0.8 copy.37
  174.4 0.4 all-reduce.2.cloned.1.call-done
  174.8 6.3 %multiply_convert_fusion = bf16[30,128,512]{2,1,0:T(8,128)(2,1)} fusion(f32[30,128,512]{2,1,0:T(8,128)} %all-reduce.2.cloned.1.call-done), kind=kLoop, calls=%fused_computation.12 | loop fusion | flops 3932160 | bytes 11796480 | tf_op jit(solution)/shard_map/convert_element_type | solution.py:49
  (6 shorter events, 0.1 us)
Async XLA Ops:
  7.2 18.1 %copy-start = (bf16[64,128,128]{2,1,0:T(8,128)(2,1)S(1)}, bf16[64,128,128]{2,1,0:T(8,128)(2,1)}, u32[]{:S(2)}) copy-start(bf16[64,128,128]{2,1,0:T(8,128)(2,1)} %param.11) | copy-start | bytes 6291460
  7.2 15.9 %copy-start.1 = (bf16[1024,128]{1,0:T(8,128)(2,1)S(1)}, bf16[1024,128]{1,0:T(8,128)(2,1)}, u32[]{:S(2)}) copy-start(bf16[1024,128]{1,0:T(8,128)(2,1)} %param.10) | copy-start | bytes 786436
  7.2 35.3 %all-gather.2.cloned.1.call-start = ((), (), s32[]{:S(2)}) async-start(), calls=%async_computation.3 | async-start | bytes 1310720 | tf_op jit(solution)/shard_map/all_gather | solution.py:41
  10.8 12.3 %all-to-all-start = ((bf16[8,1,128,128]{2,3,1,0:T(8,128)(2,1)}), bf16[8,1,128,128]{2,3,1,0:T(8,128)(2,1)S(1)}, u32[]{:S(2)}, u32[]{:S(2)}) async-start(bf16[8,1,128,128]{2,3,1,0:T(8,128)(2,1)} %bitcast.6), calls=%async_computation | async-start | bytes 524288 | tf_op jit(solution)/shard_map/all_to_all | solution.py:23
  16.0 158.8 %all-reduce.2.cloned.1.call-start = ((), (), s32[]{:S(2)}) async-start(), calls=%async_computation.4 | async-start | bytes 15728640 | tf_op jit(solution)/shard_map/psum | solution.py:48
  96.5 21.5 %all-to-all-start.2 = ((bf16[8,1,128,128]{3,2,1,0:T(8,128)(2,1)}), bf16[8,1,128,128]{3,2,1,0:T(8,128)(2,1)S(1)}, u32[]{:S(2)}, u32[]{:S(2)}) async-start(bf16[8,1,128,128]{3,2,1,0:T(8,128)(2,1)} %fusion.23), calls=%async_computation.2 | async-start | bytes 524288 | tf_op jit(solution)/shard_map/all_to_all | solution.py:73
  118.0 9.4 %copy-start.2 = (bf16[128,512]{1,0:T(8,128)(2,1)S(1)}, bf16[128,512]{1,0:T(8,128)(2,1)}, u32[]{:S(2)}) copy-start(bf16[128,512]{1,0:T(8,128)(2,1)} %param.18) | copy-start | bytes 393220
  118.0 53.7 %all-to-all-start.1 = ((f32[4,128,1024]{2,1,0:T(8,128)}), f32[4,128,1024]{2,1,0:T(8,128)}, u32[]{:S(2)}, u32[]{:S(2)}) async-start(f32[4,128,1024]{2,1,0:T(8,128)} %add.33), calls=%async_computation.1 | async-start | bytes 4194304 | tf_op jit(solution)/shard_map/all_to_all | solution.py:56
Sparse Core Ops, SparseCore 0:
  9.6 32.8 all-gather.1
  51.4 123.2 all-reduce.1

commit v4 on v3

--- a/solution.py
+++ b/solution.py
@@ -35,19 +35,19 @@
     )
     block_coef = coef[block_rel]
     summed = jnp.einsum(
-        "ki,kb,kca->bica", row_select, block_coef, message, precision=lax.Precision.HIGH
+        "ki,kb,kca->bcia", row_select, block_coef, message, precision=lax.Precision.HIGH
     ).astype(jnp.bfloat16)
     scale_factor = 1.0 / math.sqrt(partitions * node_count)
     grad_full = lax.all_gather(cotangent, "feat", axis=1, tiled=True).reshape(
         owned_blocks, blk_size, full_width
     )
-    basis_part = jnp.einsum("bica,iae->bce", summed, grad_full, preferred_element_type=jnp.float32)
+    basis_part = jnp.einsum("bcia,iae->bce", summed, grad_full, preferred_element_type=jnp.float32)
     basis_part, summed, grad_full, bases = lax.optimization_barrier(
         (basis_part, summed, grad_full, bases)
     )
     basis_total = lax.psum(basis_part, "node")
     basis_grad = (basis_total * scale_factor).astype(jnp.bfloat16)
-    combined = jnp.einsum("bica,bco->oia", summed, bases, preferred_element_type=jnp.float32)
+    combined = jnp.einsum("bcia,bco->oia", summed, bases, preferred_element_type=jnp.float32)
     feat_parts = lax.axis_size("feat")
     out_cols = full_width // feat_parts
     combined = combined.reshape(feat_parts, out_cols, node_count) + jnp.einsum(

time: 189 us -> 189 us (level)
  no operation moved by 1% of the time
where the time goes in v4:
time: 189 us; the launch traced here: 188 us
  matrix products  72.8 us (39%)
  waiting for transfers between devices  45.7 us (24%)
  other arithmetic  27.1 us (14%)
  local copies, waits for them, and re-layouts  14.9 us (8%)
  between operations  14.1 us (7%)
  starting transfers between devices  13.3 us (7%)
    all_to_all x1, waiting for transfers between devices, body(): lax.all_to_all(combined, 'feat', split_axis=0, concat_axis=0, tiled=True)  41.9 us
    dot_general x1, matrix products, body(): jnp.einsum('ki,kb,bica->kca', row_select, block_coef, grad_summed, precis...  23.1 us
    dot_general x1, matrix products, body(): jnp.einsum('ki,kb,kca->bcia', row_select, block_coef, message, precision=...  11.2 us
    dot_general x1, matrix products, body(): jnp.einsum('bcia,iae->bce', summed, grad_full, preferred_element_type=jnp...  8.79 us
    scatter-add x1, other arithmetic, body(): jnp.zeros((slot_count_total,) + grad_source.shape[1:], jnp.float32)  8.79 us
    dot_general x1, matrix products, body(): jnp.einsum('bcia,bco->oia', summed, bases, preferred_element_type=jnp.flo...  8.75 us
    dot_general x1, matrix products, body(): jnp.einsum('iae,bce->bica', grad_full, bases, preferred_element_type=jnp....  6.8 us
    convert_element_type x1, other arithmetic, body(): basis_grad = (basis_total * scale_factor).astype(jnp.bfloat16)  6.35 us
  transfers between devices with their start and end apart: 5, of which 3 were waited for; matrix products, arithmetic and copies ran while one was open for 53% of the time, Pallas kernels for 0%

profile of v4, /device:TPU:0, one launch (start us, length us, event | category | flops | bytes accessed | tf_op | source)
XLA Modules:
  0.0 187.9 jit_solution(15552285900118686268)
XLA Ops:
  7.2 0.0 copy-start
  7.2 0.0 copy-start.1
  7.2 0.0 all-gather.2.cloned.1.call-start
  7.2 0.7 all-gather.2.cloned.1.call-update
  7.9 0.7 fusion.29
  8.6 2.2 %gather_fusion.1 = bf16[8,128,128]{1,2,0:T(8,128)(2,1)} fusion(bf16[8,128,128]{1,2,0:T(8,128)(2,1)} %bitcast.70, s32[1024]{0:T(1024)S(1)} %pad_clamp_fusion.1), kind=kCustom, calls=%fused_computation.1 | custom fusion | bytes 524320 | tf_op jit(solution)/shard_map/gather | solution.py:22
  10.8 5.2 %all-to-all-start = ((bf16[8,1,128,128]{2,3,1,0:T(8,128)(2,1)}), bf16[8,1,128,128]{2,3,1,0:T(8,128)(2,1)S(1)}, u32[]{:S(2)}, u32[]{:S(2)}) async-start(bf16[8,1,128,128]{2,3,1,0:T(8,128)(2,1)} %bitcast.6), calls=%async_computation | async-start | bytes 524288 | tf_op jit(solution)/shard_map/all_to_all | solution.py:23
  16.0 0.0 all-reduce.2.cloned.1.call-start
  16.0 0.7 compare_select_fusion
  16.7 0.7 fusion.28
  17.4 2.8 %fusion.31 = f32[512,1024]{1,0:T(8,128)} fusion(bf16[128,512]{1,0:T(8,128)(2,1)} %param.18, bf16[1024,128]{1,0:T(8,128)(2,1)} %param.10), kind=kOutput, calls=%fused_computation.46 | convolution fusion | flops 134217728 | bytes 2490368 | tf_op jit(solution)/shard_map/nc,co->on/dot_general | solution.py:53
  20.2 0.7 compare_select_fusion.2
  20.9 0.9 copy.25
  21.8 0.6 gather_fusion
  22.4 0.1 copy.26
  22.4 0.7 multiply_bitcast_fusion.1
  23.1 0.0 all-to-all-done
  23.1 0.0 copy-done.1
  23.2 2.1 %gather_fusion.2 = bf16[64,128,128]{1,2,0:T(8,128)(2,1)} fusion(bf16[16,128,128]{1,2,0:T(8,128)(2,1)S(1)} %pad_maximum_fusion, s32[1024]{0:T(1024)S(1)} %pad_clamp_fusion), kind=kCustom, calls=%fused_computation.2 | custom fusion | bytes 4194560 | tf_op jit(solution)/shard_map/gather | solution.py:28
  25.3 0.0 copy-done
  25.3 3.2 %fusion.30 = f32[64,128,128]{2,1,0:T(8,128)S(1)} fusion(bf16[64,128,128]{1,2,0:T(8,128)(2,1)} %gather_fusion.2, bf16[64,128,128]{2,1,0:T(8,128)(2,1)S(1)} %copy-done), kind=kOutput, calls=%fused_computation.45 | convolution fusion | flops 268435456 | bytes 8388608 | tf_op jit(solution)/shard_map/kab,kcb->kca/dot_general | solution.py:29
  28.5 11.2 %convert_bitcast_fusion = bf16[30,128,8,128]{3,2,1,0:T(8,128)(2,1)} fusion(f32[64,128,128]{2,1,0:T(8,128)S(1)} %fusion.30, f32[64,8]{0,1:T(8,128)S(1)} %fusion.28, f32[64,30]{0,1:T(8,128)S(1)} %copy.26), kind=kOutput, calls=%fused_computation.13 | convolution fusion | flops 1513896960 | bytes 12068352 | tf_op jit(solution)/shard_map/ki,kb,kca->bcia/dot_general | solution.py:37
  39.7 2.8 %all-gather.2.cloned.1.call-done = bf16[1024,512]{1,0:T(8,128)(2,1)} async-done(((bf16[1024,128]{1,0:T(8,128)(2,1)}), bf16[1024,512]{1,0:T(8,128)(2,1)}) %all-gather.2.cloned.1.call-update) | async-done | bytes 1048592 | tf_op jit(solution)/shard_map/all_gather | solution.py:41
  42.5 8.8 %fusion.10 = f32[30,128,512]{2,1,0:T(8,128)} fusion(bf16[8,128,512,1]{2,1,0,3:T(8,128)(2,1)} %bitcast.73, bf16[30,128,8,128]{3,2,1,0:T(8,128)(2,1)} %convert_bitcast_fusion), kind=kOutput, calls=%fused_computation.19 | convolution fusion | flops 4026531840 | bytes 16777216 | tf_op jit(solution)/shard_map/bcia,iae->bce/dot_general | solution.py:44
  51.3 0.0 all-reduce.2.cloned.1.call-update
  51.3 6.8 %convolution_bitcast_fusion = f32[30,8,128,128]{3,2,1,0:T(8,128)S(1)} fusion(bf16[30,128,512]{2,1,0:T(8,128)(2,1)} %param.17, bf16[8,128,512]{2,1,0:T(8,128)(2,1)} %bitcast.74), kind=kOutput, calls=%fused_computation.7 | convolution fusion | flops 4026531840 | bytes 20709376 | tf_op jit(solution)/shard_map/iae,bce->bica/dot_general | solution.py:58
  58.1 23.1 %bitcast_convert_fusion = bf16[64,128,128]{2,0,1:T(8,128)(2,1)} fusion(f32[30,8,128,128]{3,2,1,0:T(8,128)S(1)} %convolution_bitcast_fusion, f32[64,30,8,1]{0,2,1,3:T(8,128)} %multiply_bitcast_fusion.1), kind=kOutput, calls=%fused_computation.14 | convolution fusion | flops 1510998016 | bytes 17887232 | tf_op jit(solution)/shard_map/ki,kb,bica->kca/dot_general | solution.py:59
  81.2 5.6 %fusion.15 = f32[64,128,128]{2,1,0:T(8,128)} fusion(bf16[64,128,128]{2,1,0:T(8,128)(2,1)S(1)} %copy-done, bf16[64,128,128]{2,0,1:T(8,128)(2,1)} %bitcast_convert_fusion), kind=kOutput, calls=%fused_computation.20 | convolution fusion | flops 268435456 | bytes 8388608 | tf_op jit(solution)/shard_map/kab,kca->kcb/dot_general | solution.py:62
  86.8 0.1 broadcast_in_dim.20
  86.9 8.8 %scatter_fusion = f32[16,128,128]{2,1,0:T(8,128)S(1)} fusion(f32[16,128,128]{2,1,0:T(8,128)S(1)} %broadcast_in_dim.20, s32[64]{0:T(128)S(1)} %compare_select_fusion, f32[64,128,128]{2,1,0:T(8,128)} %fusion.15), kind=kCustom, calls=%fused_computation.3 | custom fusion | flops 1048576 | bytes 12583168 | tf_op jit(solution)/shard_map/scatter-add | solution.py:68
  95.7 0.7 fusion.23
  96.5 3.4 %all-to-all-start.2 = ((bf16[8,1,128,128]{3,2,1,0:T(8,128)(2,1)}), bf16[8,1,128,128]{3,2,1,0:T(8,128)(2,1)S(1)}, u32[]{:S(2)}, u32[]{:S(2)}) async-start(bf16[8,1,128,128]{3,2,1,0:T(8,128)(2,1)} %fusion.23), calls=%async_computation.2 | async-start | bytes 524288 | tf_op jit(solution)/shard_map/all_to_all | solution.py:73
  99.9 8.8 %fusion.17 = f32[512,8,128]{2,0,1:T(8,128)S(1)} fusion(bf16[30,128,8,128]{3,2,1,0:T(8,128)(2,1)} %convert_bitcast_fusion, bf16[30,128,512]{2,1,0:T(8,128)(2,1)} %param.17), kind=kOutput, calls=%fused_computation.22 | convolution fusion | flops 4026531840 | bytes 13893632 | tf_op jit(solution)/shard_map/bcia,bco->oia/dot_general | solution.py:50
  108.7 2.5 %copy.32 = f32[512,8,128]{2,1,0:T(8,128)} copy(f32[512,8,128]{2,0,1:T(8,128)S(1)} %fusion.17) | data formatting | bytes 4194304 | tf_op jit(solution)/shard_map/bcia,bco->oia/dot_general | solution.py:50
  111.2 2.7 %reshape.37 = f32[4,128,1024]{2,1,0:T(8,128)} reshape(f32[512,8,128]{2,1,0:T(8,128)} %copy.32) | data formatting | bytes 4194304 | tf_op jit(solution)/shard_map/reshape | solution.py:53
  113.9 4.1 %add.33 = f32[4,128,1024]{2,1,0:T(8,128)} add(f32[4,128,1024]{2,1,0:T(8,128)} %reshape.37, f32[4,128,1024]{2,1,0:T(8,128)} %bitcast.69) | non-fusion elementwise | flops 524288 | bytes 6291456 | tf_op jit(solution)/shard_map/add | solution.py:53
  118.0 0.0 all-to-all-done.2
  118.0 4.7 %all-to-all-start.1 = ((f32[4,128,1024]{2,1,0:T(8,128)}), f32[4,128,1024]{2,1,0:T(8,128)}, u32[]{:S(2)}, u32[]{:S(2)}) async-start(f32[4,128,1024]{2,1,0:T(8,128)} %add.33), calls=%async_computation.1 | async-start | bytes 4194304 | tf_op jit(solution)/shard_map/all_to_all | solution.py:56
  122.7 0.8 slice.15
  123.5 2.6 %scatter_fusion.1 = f32[8,128,128]{2,1,0:T(8,128)} fusion(f32[8,128,128]{2,1,0:T(8,128)} %slice.15, s32[8]{0:T(128)S(1)} %fusion.29, f32[8,128,128]{2,1,0:T(8,128)S(1)} %bitcast_convert_fusion.1), kind=kCustom, calls=%fused_computation.4 | custom fusion | flops 131072 | bytes 1572896 | tf_op jit(solution)/shard_map/scatter-add | solution.py:82
  126.2 1.2 copy.36
  127.4 0.0 copy-done.2
  127.4 2.5 %convolution_add_fusion = f32[8,128,128]{2,1,0:T(8,128)} fusion(bf16[8,128,512]{2,1,0:T(8,128)(2,1)} %bitcast.75, f32[8,128,128]{1,2,0:T(8,128)S(1)} %copy.36, bf16[128,512]{1,0:T(8,128)(2,1)S(1)} %copy-done.2), kind=kOutput, calls=%fused_computation.23 | convolution fusion | flops 134348800 | bytes 2228224 | tf_op jit(solution)/shard_map/iae,ce->iac/dot_general | solution.py:86
  129.9 41.9 %all-to-all-done.1 = f32[4,128,1024]{2,1,0:T(8,128)} async-done(((f32[4,128,1024]{2,1,0:T(8,128)}), f32[4,128,1024]{2,1,0:T(8,128)}, u32[]{:S(2)}, u32[]{:S(2)}) %all-to-all-start.1) | async-done | bytes 2097184 | tf_op jit(solution)/shard_map/all_to_all | solution.py:56
  171.7 1.8 reduce_sum.9
  173.6 0.8 copy.37
  174.4 0.4 all-reduce.2.cloned.1.call-done
  174.8 6.3 %multiply_convert_fusion = bf16[30,128,512]{2,1,0:T(8,128)(2,1)} fusion(f32[30,128,512]{2,1,0:T(8,128)} %all-reduce.2.cloned.1.call-done), kind=kLoop, calls=%fused_computation.12 | loop fusion | flops 3932160 | bytes 11796480 | tf_op jit(solution)/shard_map/convert_element_type | solution.py:49
  (6 shorter events, 0.1 us)
Async XLA Ops:
  7.2 18.1 %copy-start = (bf16[64,128,128]{2,1,0:T(8,128)(2,1)S(1)}, bf16[64,128,128]{2,1,0:T(8,128)(2,1)}, u32[]{:S(2)}) copy-start(bf16[64,128,128]{2,1,0:T(8,128)(2,1)} %param.11) | copy-start | bytes 6291460
  7.2 15.9 %copy-start.1 = (bf16[1024,128]{1,0:T(8,128)(2,1)S(1)}, bf16[1024,128]{1,0:T(8,128)(2,1)}, u32[]{:S(2)}) copy-start(bf16[1024,128]{1,0:T(8,128)(2,1)} %param.10) | copy-start | bytes 786436
  7.2 35.3 %all-gather.2.cloned.1.call-start = ((), (), s32[]{:S(2)}) async-start(), calls=%async_computation.3 | async-start | bytes 1310720 | tf_op jit(solution)/shard_map/all_gather | solution.py:41
  10.8 12.3 %all-to-all-start = ((bf16[8,1,128,128]{2,3,1,0:T(8,128)(2,1)}), bf16[8,1,128,128]{2,3,1,0:T(8,128)(2,1)S(1)}, u32[]{:S(2)}, u32[]{:S(2)}) async-start(bf16[8,1,128,128]{2,3,1,0:T(8,128)(2,1)} %bitcast.6), calls=%async_computation | async-start | bytes 524288 | tf_op jit(solution)/shard_map/all_to_all | solution.py:23
  16.0 158.8 %all-reduce.2.cloned.1.call-start = ((), (), s32[]{:S(2)}) async-start(), calls=%async_computation.4 | async-start | bytes 15728640 | tf_op jit(solution)/shard_map/psum | solution.py:48
  96.5 21.5 %all-to-all-start.2 = ((bf16[8,1,128,128]{3,2,1,0:T(8,128)(2,1)}), bf16[8,1,128,128]{3,2,1,0:T(8,128)(2,1)S(1)}, u32[]{:S(2)}, u32[]{:S(2)}) async-start(bf16[8,1,128,128]{3,2,1,0:T(8,128)(2,1)} %fusion.23), calls=%async_computation.2 | async-start | bytes 524288 | tf_op jit(solution)/shard_map/all_to_all | solution.py:73
  118.0 9.4 %copy-start.2 = (bf16[128,512]{1,0:T(8,128)(2,1)S(1)}, bf16[128,512]{1,0:T(8,128)(2,1)}, u32[]{:S(2)}) copy-start(bf16[128,512]{1,0:T(8,128)(2,1)} %param.18) | copy-start | bytes 393220
  118.0 53.7 %all-to-all-start.1 = ((f32[4,128,1024]{2,1,0:T(8,128)}), f32[4,128,1024]{2,1,0:T(8,128)}, u32[]{:S(2)}, u32[]{:S(2)}) async-start(f32[4,128,1024]{2,1,0:T(8,128)} %add.33), calls=%async_computation.1 | async-start | bytes 4194304 | tf_op jit(solution)/shard_map/all_to_all | solution.py:56
Sparse Core Ops, SparseCore 0:
  9.6 32.8 all-gather.1
  51.4 123.2 all-reduce.1

commit v5 on v4

--- a/solution.py
+++ b/solution.py
@@ -57,7 +57,7 @@
     layer_out = jnp.transpose(layer_cols).astype(jnp.bfloat16)
     grad_summed = jnp.einsum("iae,bce->bica", grad_full, bases, preferred_element_type=jnp.float32)
     grad_message = jnp.einsum(
-        "ki,kb,bica->kca", row_select, block_coef, grad_summed, precision=lax.Precision.HIGH
+        "ki,kb,bica->kca", row_select, block_coef, grad_summed, preferred_element_type=jnp.float32
     ).astype(jnp.bfloat16)
     grad_source = jnp.einsum(
         "kab,kca->kcb", tiles, grad_message, preferred_element_type=jnp.float32

time: 189 us -> 221 us (1.17)
  waiting for transfers between devices: 45.7 us -> 102 us
  matrix products: 72.8 us -> 51.8 us
    psum x1, waiting for transfers between devices: 0.36 us -> 50.9 us  [body(): basis_total = lax.psum(basis_part, 'node')]
    dot_general x1, matrix products: 23.1 us -> 4.86 us  [body(): jnp.einsum('ki,kb,bica->kca', row_select, block_coef, grad_summed, prefer...]
    all_to_all x1, waiting for transfers between devices: 41.9 us -> 46.7 us  [body(): lax.all_to_all(combined, 'feat', split_axis=0, concat_axis=0, tiled=True)]
  transfers between devices with their start and end apart: 5 -> 5, of which waited for: 3 -> 4; matrix products, arithmetic and copies ran while one was open for 53% -> 22% of each run, Pallas kernels for 0% -> 0%
where the time goes in v5:
time: 221 us; the launch traced here: 220 us
  waiting for transfers between devices  102 us (46%)
  matrix products  51.8 us (23%)
  other arithmetic  25 us (11%)
  between operations  14.2 us (6%)
  starting transfers between devices  13.5 us (6%)
  local copies, waits for them, and re-layouts  13.1 us (6%)
    psum x1, waiting for transfers between devices, body(): basis_total = lax.psum(basis_part, 'node')  50.9 us
    all_to_all x1, waiting for transfers between devices, body(): lax.all_to_all(combined, 'feat', split_axis=0, concat_axis=0, tiled=True)  46.7 us
    dot_general x1, matrix products, body(): jnp.einsum('ki,kb,kca->bcia', row_select, block_coef, message, precision=...  11 us
    dot_general x1, matrix products, body(): jnp.einsum('bcia,iae->bce', summed, grad_full, preferred_element_type=jnp...  9.64 us
    scatter-add x1, other arithmetic, body(): jnp.zeros((slot_count_total,) + grad_source.shape[1:], jnp.float32)  8.8 us
    dot_general x1, matrix products, body(): jnp.einsum('bcia,bco->oia', summed, bases, preferred_element_type=jnp.flo...  8.66 us
    convert_element_type x1, other arithmetic, body(): basis_grad = (basis_total * scale_factor).astype(jnp.bfloat16)  6.35 us
    dot_general x1, matrix products, body(): jnp.einsum('iae,bce->bica', grad_full, bases, preferred_element_type=jnp....  6.25 us
  transfers between devices with their start and end apart: 5, of which 4 were waited for; matrix products, arithmetic and copies ran while one was open for 22% of the time, Pallas kernels for 0%

profile of v5, /device:TPU:0, one launch (start us, length us, event | category | flops | bytes accessed | tf_op | source)
XLA Modules:
  0.0 219.9 jit_solution(16680476505139652940)
XLA Ops:
  7.2 0.0 copy-start
  7.2 0.0 copy-start.2
  7.2 0.0 all-gather.2.cloned.1.call-start
  7.2 0.7 all-gather.2.cloned.1.call-update
  7.9 0.7 fusion.29
  8.6 2.2 %gather_fusion.1 = bf16[8,128,128]{1,2,0:T(8,128)(2,1)} fusion(bf16[8,128,128]{1,2,0:T(8,128)(2,1)} %bitcast.70, s32[1024]{0:T(1024)S(1)} %pad_clamp_fusion.1), kind=kCustom, calls=%fused_computation.1 | custom fusion | bytes 524320 | tf_op jit(solution)/shard_map/gather | solution.py:22
  10.8 5.2 %all-to-all-start = ((bf16[8,1,128,128]{2,3,1,0:T(8,128)(2,1)}), bf16[8,1,128,128]{2,3,1,0:T(8,128)(2,1)S(1)}, u32[]{:S(2)}, u32[]{:S(2)}) async-start(bf16[8,1,128,128]{2,3,1,0:T(8,128)(2,1)} %bitcast.6), calls=%async_computation | async-start | bytes 524288 | tf_op jit(solution)/shard_map/all_to_all | solution.py:23
  16.0 0.7 compare_select_fusion
  16.7 0.7 fusion.28
  17.3 2.9 %fusion.31 = f32[512,1024]{1,0:T(8,128)} fusion(bf16[128,512]{1,0:T(8,128)(2,1)} %param.18, bf16[1024,128]{1,0:T(8,128)(2,1)} %param.10), kind=kOutput, calls=%fused_computation.46 | convolution fusion | flops 134217728 | bytes 2490368 | tf_op jit(solution)/shard_map/nc,co->on/dot_general | solution.py:53
  20.2 0.7 compare_select_fusion.2
  20.9 0.9 copy.25
  21.7 0.6 gather_fusion
  22.3 0.1 copy.26
  22.4 0.5 all-to-all-done
  22.9 0.0 copy-done.2
  23.0 2.1 gather_fusion.2
  25.1 0.0 copy-done
  25.1 3.2 %fusion.30 = f32[64,128,128]{2,1,0:T(8,128)S(1)} fusion(bf16[64,128,128]{1,2,0:T(8,128)(2,1)} %gather_fusion.2, bf16[64,128,128]{2,1,0:T(8,128)(2,1)S(1)} %copy-done), kind=kOutput, calls=%fused_computation.45 | convolution fusion | flops 268435456 | bytes 8388608 | tf_op jit(solution)/shard_map/kab,kcb->kca/dot_general | solution.py:29
  28.3 11.0 %convert_bitcast_fusion = bf16[30,128,8,128]{3,2,1,0:T(8,128)(2,1)} fusion(f32[64,128,128]{2,1,0:T(8,128)S(1)} %fusion.30, f32[64,8]{0,1:T(8,128)S(1)} %fusion.28, f32[64,30]{0,1:T(8,128)S(1)} %copy.26), kind=kOutput, calls=%fused_computation.13 | convolution fusion | flops 1513896960 | bytes 12068352 | tf_op jit(solution)/shard_map/ki,kb,kca->bcia/dot_general | solution.py:37
  39.4 3.1 %all-gather.2.cloned.1.call-done = bf16[1024,512]{1,0:T(8,128)(2,1)} async-done(((bf16[1024,128]{1,0:T(8,128)(2,1)}), bf16[1024,512]{1,0:T(8,128)(2,1)}) %all-gather.2.cloned.1.call-update) | async-done | bytes 1048592 | tf_op jit(solution)/shard_map/all_gather | solution.py:41
  42.5 9.6 %fusion.10 = f32[30,128,512]{2,1,0:T(8,128)} fusion(bf16[8,128,512,1]{2,1,0,3:T(8,128)(2,1)} %bitcast.73, bf16[30,128,8,128]{3,2,1,0:T(8,128)(2,1)} %convert_bitcast_fusion), kind=kOutput, calls=%fused_computation.19 | convolution fusion | flops 4026531840 | bytes 16777216 | tf_op jit(solution)/shard_map/bcia,iae->bce/dot_general | solution.py:44
  52.2 0.0 copy-done.3
  52.2 6.2 %convolution_bitcast_fusion = bf16[30,8,128,128]{3,2,1,0:T(8,128)(2,1)S(1)} fusion(bf16[30,128,512]{2,1,0:T(8,128)(2,1)} %param.17, bf16[8,128,512]{2,1,0:T(8,128)(2,1)S(1)} %bitcast.74), kind=kOutput, calls=%fused_computation.7 | convolution fusion | flops 4026531840 | bytes 12845056 | tf_op jit(solution)/shard_map/iae,bce->bica/dot_general | solution.py:58
  58.4 4.9 %bitcast_convert_fusion = bf16[64,128,128]{2,0,1:T(8,128)(2,1)S(1)} fusion(bf16[30,8,128,128]{3,2,1,0:T(8,128)(2,1)S(1)} %convolution_bitcast_fusion, bf16[64,30,8,1]{0,2,1,3:T(8,128)(2,1)S(1)} %multiply_bitcast_fusion.1), kind=kOutput, calls=%fused_computation.14 | convolution fusion | flops 503316480 | bytes 9992192 | tf_op jit(solution)/shard_map/ki,kb,bica->kca/dot_general | solution.py:59
  63.3 4.1 %fusion.15 = f32[64,128,128]{2,1,0:T(8,128)} fusion(bf16[64,128,128]{2,1,0:T(8,128)(2,1)S(1)} %copy-done, bf16[64,128,128]{2,0,1:T(8,128)(2,1)S(1)} %bitcast_convert_fusion), kind=kOutput, calls=%fused_computation.20 | convolution fusion | flops 268435456 | bytes 8388608 | tf_op jit(solution)/shard_map/kab,kca->kcb/dot_general | solution.py:62
  67.3 0.1 broadcast_in_dim.20
  67.4 8.8 %scatter_fusion = f32[16,128,128]{2,1,0:T(8,128)S(1)} fusion(f32[16,128,128]{2,1,0:T(8,128)S(1)} %broadcast_in_dim.20, s32[64]{0:T(128)S(1)} %compare_select_fusion, f32[64,128,128]{2,1,0:T(8,128)} %fusion.15), kind=kCustom, calls=%fused_computation.3 | custom fusion | flops 1048576 | bytes 12583168 | tf_op jit(solution)/shard_map/scatter-add | solution.py:68
  76.2 0.7 fusion.23
  77.0 3.4 %all-to-all-start.2 = ((bf16[8,1,128,128]{3,2,1,0:T(8,128)(2,1)}), bf16[8,1,128,128]{3,2,1,0:T(8,128)(2,1)S(1)}, u32[]{:S(2)}, u32[]{:S(2)}) async-start(bf16[8,1,128,128]{3,2,1,0:T(8,128)(2,1)} %fusion.23), calls=%async_computation.2 | async-start | bytes 524288 | tf_op jit(solution)/shard_map/all_to_all | solution.py:73
  80.4 0.3 all-reduce.2.cloned.1.call-start
  80.7 0.5 all-reduce.2.cloned.1.call-update
  81.2 8.7 %fusion.17 = f32[512,8,128]{2,0,1:T(8,128)S(1)} fusion(bf16[30,128,8,128]{3,2,1,0:T(8,128)(2,1)} %convert_bitcast_fusion, bf16[30,128,512]{2,1,0:T(8,128)(2,1)} %param.17), kind=kOutput, calls=%fused_computation.22 | convolution fusion | flops 4026531840 | bytes 13893632 | tf_op jit(solution)/shard_map/bcia,bco->oia/dot_general | solution.py:50
  89.8 2.5 %copy.32 = f32[512,8,128]{2,1,0:T(8,128)} copy(f32[512,8,128]{2,0,1:T(8,128)S(1)} %fusion.17) | data formatting | bytes 4194304 | tf_op jit(solution)/shard_map/bcia,bco->oia/dot_general | solution.py:50
  92.4 2.7 %reshape.37 = f32[4,128,1024]{2,1,0:T(8,128)} reshape(f32[512,8,128]{2,1,0:T(8,128)} %copy.32) | data formatting | bytes 4194304 | tf_op jit(solution)/shard_map/reshape | solution.py:53
  95.1 4.1 %add.33 = f32[4,128,1024]{2,1,0:T(8,128)} add(f32[4,128,1024]{2,1,0:T(8,128)} %reshape.37, f32[4,128,1024]{2,1,0:T(8,128)} %bitcast.69) | non-fusion elementwise | flops 524288 | bytes 6291456 | tf_op jit(solution)/shard_map/add | solution.py:53
  99.2 0.0 all-to-all-done.2
  99.2 4.6 %all-to-all-start.1 = ((f32[4,128,1024]{2,1,0:T(8,128)}), f32[4,128,1024]{2,1,0:T(8,128)}, u32[]{:S(2)}, u32[]{:S(2)}) async-start(f32[4,128,1024]{2,1,0:T(8,128)} %add.33), calls=%async_computation.1 | async-start | bytes 4194304 | tf_op jit(solution)/shard_map/all_to_all | solution.py:56
  103.9 1.0 scatter_fusion.1
  104.9 0.2 copy.36
  105.1 0.0 copy-done.4
  105.1 1.2 convolution_add_fusion
  106.3 46.7 %all-to-all-done.1 = f32[4,128,1024]{2,1,0:T(8,128)} async-done(((f32[4,128,1024]{2,1,0:T(8,128)}), f32[4,128,1024]{2,1,0:T(8,128)}, u32[]{:S(2)}, u32[]{:S(2)}) %all-to-all-start.1) | async-done | bytes 2097184 | tf_op jit(solution)/shard_map/all_to_all | solution.py:56
  153.0 2.0 reduce_sum.9
  155.0 0.0 copy-start.1
  155.0 0.8 copy.37
  155.9 50.9 %all-reduce.2.cloned.1.call-done = f32[30,128,512]{2,1,0:T(8,128)} async-done(((f32[30,128,512]{2,1,0:T(8,128)}), f32[30,128,512]{2,1,0:T(8,128)}) %all-reduce.2.cloned.1.call-update) | async-done | bytes 7864336 | tf_op jit(solution)/shard_map/psum | solution.py:48
  206.8 6.3 %multiply_convert_fusion = bf16[30,128,512]{2,1,0:T(8,128)(2,1)} fusion(f32[30,128,512]{2,1,0:T(8,128)} %all-reduce.2.cloned.1.call-done), kind=kLoop, calls=%fused_computation.12 | loop fusion | flops 3932160 | bytes 11796480 | tf_op jit(solution)/shard_map/convert_element_type | solution.py:49
  (10 shorter events, 0.2 us)
Async XLA Ops:
  7.2 18.0 %copy-start = (bf16[64,128,128]{2,1,0:T(8,128)(2,1)S(1)}, bf16[64,128,128]{2,1,0:T(8,128)(2,1)}, u32[]{:S(2)}) copy-start(bf16[64,128,128]{2,1,0:T(8,128)(2,1)} %param.11) | copy-start | bytes 6291460
  7.2 15.8 %copy-start.2 = (bf16[1024,128]{1,0:T(8,128)(2,1)S(1)}, bf16[1024,128]{1,0:T(8,128)(2,1)}, u32[]{:S(2)}) copy-start(bf16[1024,128]{1,0:T(8,128)(2,1)} %param.10) | copy-start | bytes 786436
  7.2 35.3 %all-gather.2.cloned.1.call-start = ((), (), s32[]{:S(2)}) async-start(), calls=%async_computation.3 | async-start | bytes 1310720 | tf_op jit(solution)/shard_map/all_gather | solution.py:41
  10.8 12.1 %all-to-all-start = ((bf16[8,1,128,128]{2,3,1,0:T(8,128)(2,1)}), bf16[8,1,128,128]{2,3,1,0:T(8,128)(2,1)S(1)}, u32[]{:S(2)}, u32[]{:S(2)}) async-start(bf16[8,1,128,128]{2,3,1,0:T(8,128)(2,1)} %bitcast.6), calls=%async_computation | async-start | bytes 524288 | tf_op jit(solution)/shard_map/all_to_all | solution.py:23
  42.5 9.6 %copy-start.3 = (bf16[1024,512]{1,0:T(8,128)(2,1)S(1)}, bf16[1024,512]{1,0:T(8,128)(2,1)}, u32[]{:S(2)}) copy-start(bf16[1024,512]{1,0:T(8,128)(2,1)} %all-gather.2.cloned.1.call-done) | copy-start | bytes 3145732
  77.0 22.2 %all-to-all-start.2 = ((bf16[8,1,128,128]{3,2,1,0:T(8,128)(2,1)}), bf16[8,1,128,128]{3,2,1,0:T(8,128)(2,1)S(1)}, u32[]{:S(2)}, u32[]{:S(2)}) async-start(bf16[8,1,128,128]{3,2,1,0:T(8,128)(2,1)} %fusion.23), calls=%async_computation.2 | async-start | bytes 524288 | tf_op jit(solution)/shard_map/all_to_all | solution.py:73
  80.4 126.3 %all-reduce.2.cloned.1.call-start = ((), (), s32[]{:S(2)}) async-start(), calls=%async_computation.4 | async-start | bytes 15728640 | tf_op jit(solution)/shard_map/psum | solution.py:48
  99.2 5.9 %copy-start.4 = (bf16[128,512]{1,0:T(8,128)(2,1)S(1)}, bf16[128,512]{1,0:T(8,128)(2,1)}, u32[]{:S(2)}) copy-start(bf16[128,512]{1,0:T(8,128)(2,1)} %param.18) | copy-start | bytes 393220
  99.2 53.8 %all-to-all-start.1 = ((f32[4,128,1024]{2,1,0:T(8,128)}), f32[4,128,1024]{2,1,0:T(8,128)}, u32[]{:S(2)}, u32[]{:S(2)}) async-start(f32[4,128,1024]{2,1,0:T(8,128)} %add.33), calls=%async_computation.1 | async-start | bytes 4194304 | tf_op jit(solution)/shard_map/all_to_all | solution.py:56
  155.0 58.1 %copy-start.1 = (bf16[64,128,128]{2,1,0:T(8,128)(2,1)S(1)}, bf16[64,128,128]{2,1,0:T(8,128)(2,1)}, u32[]{:S(2)}) copy-start(bf16[64,128,128]{2,1,0:T(8,128)(2,1)} %param.11) | copy-start | bytes 6291460
Sparse Core Ops, SparseCore 0:
  9.6 32.8 all-gather.1
  84.6 122.1 all-reduce.1

commit v6 on v4

--- a/solution.py
+++ b/solution.py
@@ -38,10 +38,13 @@
         "ki,kb,kca->bcia", row_select, block_coef, message, precision=lax.Precision.HIGH
     ).astype(jnp.bfloat16)
     scale_factor = 1.0 / math.sqrt(partitions * node_count)
-    grad_full = lax.all_gather(cotangent, "feat", axis=1, tiled=True).reshape(
-        owned_blocks, blk_size, full_width
+    feat_count = lax.axis_size("feat")
+    grad_full = lax.all_gather(cotangent, "feat", axis=0).reshape(
+        feat_count, owned_blocks, blk_size, full_width // feat_count
     )
-    basis_part = jnp.einsum("bcia,iae->bce", summed, grad_full, preferred_element_type=jnp.float32)
+    basis_part = jnp.einsum(
+        "bcia,fiae->bcfe", summed, grad_full, preferred_element_type=jnp.float32
+    ).reshape(summed.shape[0], col_width, full_width)
     basis_part, summed, grad_full, bases = lax.optimization_barrier(
         (basis_part, summed, grad_full, bases)
     )
@@ -55,7 +58,12 @@
     ).reshape(feat_parts, out_cols, node_count)
     layer_cols = lax.all_to_all(combined, "feat", split_axis=0, concat_axis=0, tiled=True).sum(0)
     layer_out = jnp.transpose(layer_cols).astype(jnp.bfloat16)
-    grad_summed = jnp.einsum("iae,bce->bica", grad_full, bases, preferred_element_type=jnp.float32)
+    grad_summed = jnp.einsum(
+        "fiae,bcfe->bica",
+        grad_full,
+        bases.reshape(bases.shape[0], col_width, feat_count, full_width // feat_count),
+        preferred_element_type=jnp.float32,
+    )
     grad_message = jnp.einsum(
         "ki,kb,bica->kca", row_select, block_coef, grad_summed, precision=lax.Precision.HIGH
     ).astype(jnp.bfloat16)
@@ -84,7 +92,10 @@
     )
     own_grad = jnp.transpose(slot_grad[:owned_blocks] + arrived, (0, 2, 1))
     self_loop_gradient = jnp.einsum(
-        "iae,ce->iac", grad_full, self_weight, preferred_element_type=jnp.float32
+        "fiae,cfe->iac",
+        grad_full,
+        self_weight.reshape(col_width, feat_count, full_width // feat_count),
+        preferred_element_type=jnp.float32,
     )
     feature_grad = (own_grad + self_loop_gradient).reshape(node_count, col_width)
     return (layer_out, feature_grad, basis_grad)

time: 189 us -> 198 us (1.048)
  local copies, waits for them, and re-layouts: 14.9 us -> 25.9 us
  waiting for transfers between devices: 45.7 us -> 40.7 us
    reshape x0 -> x2, local copies, waits for them, and re-layouts: none -> 8.39 us  [the longest x1 7.7 us: body(): bases.reshape(bases.shape[0], col_width, feat_count, full_width // feat_c...]
    all_to_all x1, waiting for transfers between devices: 41.9 us -> 39.4 us  [body(): lax.all_to_all(combined, 'feat', split_axis=0, concat_axis=0, tiled=True)]
    all_gather x1, waiting for transfers between devices: 2.79 us -> 0.53 us  [body(): lax.all_gather(cotangent, 'feat', axis=0)]
  transfers between devices with their start and end apart: 5 -> 5, of which waited for: 3 -> 2; matrix products, arithmetic and copies ran while one was open for 53% -> 56% of each run, Pallas kernels for 0% -> 0%
where the time goes in v6:
time: 198 us; the launch traced here: 197 us
  matrix products  73.7 us (37%)
  waiting for transfers between devices  40.7 us (21%)
  other arithmetic  28.3 us (14%)
  local copies, waits for them, and re-layouts  25.9 us (13%)
  between operations  14.1 us (7%)
  starting transfers between devices  13.9 us (7%)
    all_to_all x1, waiting for transfers between devices, body(): lax.all_to_all(combined, 'feat', split_axis=0, concat_axis=0, tiled=True)  39.4 us
    dot_general x1, matrix products, body(): jnp.einsum('ki,kb,bica->kca', row_select, block_coef, grad_summed, precis...  23.1 us
    dot_general x1, matrix products, body(): jnp.einsum('ki,kb,kca->bcia', row_select, block_coef, message, precision=...  11.2 us
    dot_general x1, matrix products, body(): jnp.einsum('bcia,fiae->bcfe', summed, grad_full, preferred_element_type=j...  9.7 us
    scatter-add x1, other arithmetic, body(): jnp.zeros((slot_count_total,) + grad_source.shape[1:], jnp.float32)  8.8 us
    dot_general x1, matrix products, body(): jnp.einsum('bcia,bco->oia', summed, bases, preferred_element_type=jnp.flo...  8.75 us
    reshape x1, local copies, waits for them, and re-layouts, body(): bases.reshape(bases.shape[0], col_width, feat_count, full_width // feat_c...  7.7 us
    dot_general x1, matrix products, body(): jnp.einsum('fiae,bcfe->bica', grad_full, bases.reshape(bases.shape[0], co...  6.89 us
  transfers between devices with their start and end apart: 5, of which 2 were waited for; matrix products, arithmetic and copies ran while one was open for 56% of the time, Pallas kernels for 0%

profile of v6, /device:TPU:0, one launch (start us, length us, event | category | flops | bytes accessed | tf_op | source)
XLA Modules:
  0.0 196.5 jit_solution(11244057678219457033)
XLA Ops:
  7.2 0.0 copy-start
  7.2 0.0 copy-start.2
  7.2 0.0 all-gather.3.cloned.1.call-start
  7.2 0.7 all-gather.3.cloned.1.call-update
  7.9 0.7 fusion.31
  8.6 2.2 %gather_fusion.1 = bf16[8,128,128]{1,2,0:T(8,128)(2,1)} fusion(bf16[8,128,128]{1,2,0:T(8,128)(2,1)} %bitcast.78, s32[1024]{0:T(1024)S(1)} %pad_clamp_fusion.1), kind=kCustom, calls=%fused_computation.1 | custom fusion | bytes 524320 | tf_op jit(solution)/shard_map/gather | solution.py:22
  10.8 5.2 %all-to-all-start = ((bf16[8,1,128,128]{2,3,1,0:T(8,128)(2,1)}), bf16[8,1,128,128]{2,3,1,0:T(8,128)(2,1)S(1)}, u32[]{:S(2)}, u32[]{:S(2)}) async-start(bf16[8,1,128,128]{2,3,1,0:T(8,128)(2,1)} %bitcast.6), calls=%async_computation | async-start | bytes 524288 | tf_op jit(solution)/shard_map/all_to_all | solution.py:23
  16.0 0.0 all-reduce.2.cloned.1.call-start
  16.0 0.7 compare_select_fusion
  16.7 0.7 fusion.30
  17.4 2.8 %fusion.33 = f32[512,1024]{1,0:T(8,128)} fusion(bf16[128,512]{1,0:T(8,128)(2,1)} %param.18, bf16[1024,128]{1,0:T(8,128)(2,1)} %param.10), kind=kOutput, calls=%fused_computation.48 | convolution fusion | flops 134217728 | bytes 2490368 | tf_op jit(solution)/shard_map/nc,co->on/dot_general | solution.py:56
  20.2 0.7 compare_select_fusion.2
  20.9 0.9 copy.31
  21.7 0.6 gather_fusion
  22.3 0.1 copy.32
  22.4 0.7 multiply_bitcast_fusion.1
  23.1 0.0 all-to-all-done
  23.1 2.1 %gather_fusion.2 = bf16[64,128,128]{1,2,0:T(8,128)(2,1)} fusion(bf16[16,128,128]{1,2,0:T(8,128)(2,1)S(1)} %pad_maximum_fusion, s32[1024]{0:T(1024)S(1)} %pad_clamp_fusion), kind=kCustom, calls=%fused_computation.2 | custom fusion | bytes 4194560 | tf_op jit(solution)/shard_map/gather | solution.py:28
  25.3 3.2 %fusion.32 = f32[64,128,128]{2,1,0:T(8,128)S(1)} fusion(bf16[64,128,128]{1,2,0:T(8,128)(2,1)} %gather_fusion.2, bf16[64,128,128]{2,1,0:T(8,128)(2,1)S(1)} %copy-done), kind=kOutput, calls=%fused_computation.47 | convolution fusion | flops 268435456 | bytes 8388608 | tf_op jit(solution)/shard_map/kab,kcb->kca/dot_general | solution.py:29
  28.5 11.2 %convert_bitcast_fusion = bf16[30,128,8,128]{3,2,1,0:T(8,128)(2,1)} fusion(f32[64,128,128]{2,1,0:T(8,128)S(1)} %fusion.32, f32[64,8]{0,1:T(8,128)S(1)} %fusion.30, f32[64,30]{0,1:T(8,128)S(1)} %copy.32), kind=kOutput, calls=%fused_computation.13 | convolution fusion | flops 1513896960 | bytes 12068352 | tf_op jit(solution)/shard_map/ki,kb,kca->bcia/dot_general | solution.py:37
  39.7 0.5 all-gather.3.cloned.1.call-done
  40.3 1.6 copy.35
  41.9 9.7 %fusion.10 = f32[30,128,512]{2,1,0:T(8,128)} fusion(bf16[512,128,8,1]{1,0,2,3:T(8,128)(2,1)S(1)} %bitcast.81, bf16[30,128,8,128]{3,2,1,0:T(8,128)(2,1)} %convert_bitcast_fusion), kind=kOutput, calls=%fused_computation.19 | convolution fusion | flops 4026531840 | bytes 16777216 | tf_op jit(solution)/shard_map/bcia,fiae->bcfe/dot_general | solution.py:45
  51.6 0.0 all-reduce.2.cloned.1.call-update
  51.6 7.7 %reshape.47 = bf16[30,128,4,128]{3,2,1,0:T(4,128)(2,1)} reshape(bf16[30,128,512]{2,1,0:T(8,128)(2,1)} %param.17) | data formatting | bytes 7864320 | tf_op jit(solution)/shard_map/reshape | solution.py:64
  59.3 6.9 %convolution_bitcast_fusion = f32[30,8,128,128]{3,2,1,0:T(8,128)S(1)} fusion(bf16[30,128,4,128,1]{3,2,1,0,4:T(4,128)(2,1)} %bitcast.77, bf16[4,8,128,128]{3,2,1,0:T(8,128)(2,1)} %bitcast.75), kind=kOutput, calls=%fused_computation.7 | convolution fusion | flops 4026531840 | bytes 20709376 | tf_op jit(solution)/shard_map/fiae,bcfe->bica/dot_general | solution.py:61
  66.2 23.1 %bitcast_convert_fusion = bf16[64,128,128]{2,0,1:T(8,128)(2,1)} fusion(f32[30,8,128,128]{3,2,1,0:T(8,128)S(1)} %convolution_bitcast_fusion, f32[64,30,8,1]{0,2,1,3:T(8,128)} %multiply_bitcast_fusion.1), kind=kOutput, calls=%fused_computation.14 | convolution fusion | flops 1510998016 | bytes 17887232 | tf_op jit(solution)/shard_map/ki,kb,bica->kca/dot_general | solution.py:67
  89.3 5.6 %fusion.15 = f32[64,128,128]{2,1,0:T(8,128)} fusion(bf16[64,128,128]{2,1,0:T(8,128)(2,1)S(1)} %copy-done, bf16[64,128,128]{2,0,1:T(8,128)(2,1)} %bitcast_convert_fusion), kind=kOutput, calls=%fused_computation.20 | convolution fusion | flops 268435456 | bytes 8388608 | tf_op jit(solution)/shard_map/kab,kca->kcb/dot_general | solution.py:70
  94.9 0.1 broadcast_in_dim.20
  95.0 8.8 %scatter_fusion = f32[16,128,128]{2,1,0:T(8,128)S(1)} fusion(f32[16,128,128]{2,1,0:T(8,128)S(1)} %broadcast_in_dim.20, s32[64]{0:T(128)S(1)} %compare_select_fusion, f32[64,128,128]{2,1,0:T(8,128)} %fusion.15), kind=kCustom, calls=%fused_computation.3 | custom fusion | flops 1048576 | bytes 12583168 | tf_op jit(solution)/shard_map/scatter-add | solution.py:76
  103.8 0.7 fusion.25
  104.6 3.8 %all-to-all-start.2 = ((bf16[8,1,128,128]{3,2,1,0:T(8,128)(2,1)}), bf16[8,1,128,128]{3,2,1,0:T(8,128)(2,1)S(1)}, u32[]{:S(2)}, u32[]{:S(2)}) async-start(bf16[8,1,128,128]{3,2,1,0:T(8,128)(2,1)} %fusion.25), calls=%async_computation.2 | async-start | bytes 524288 | tf_op jit(solution)/shard_map/all_to_all | solution.py:81
  108.4 8.7 %fusion.17 = f32[512,8,128]{2,0,1:T(8,128)S(1)} fusion(bf16[30,128,8,128]{3,2,1,0:T(8,128)(2,1)} %convert_bitcast_fusion, bf16[30,128,512]{2,1,0:T(8,128)(2,1)} %param.17), kind=kOutput, calls=%fused_computation.22 | convolution fusion | flops 4026531840 | bytes 13893632 | tf_op jit(solution)/shard_map/bcia,bco->oia/dot_general | solution.py:53
  117.2 2.5 %copy.39 = f32[512,8,128]{2,1,0:T(8,128)} copy(f32[512,8,128]{2,0,1:T(8,128)S(1)} %fusion.17) | data formatting | bytes 4194304 | tf_op jit(solution)/shard_map/bcia,bco->oia/dot_general | solution.py:53
  119.7 2.9 %reshape.45 = f32[4,128,1024]{2,1,0:T(8,128)} reshape(f32[512,8,128]{2,1,0:T(8,128)} %copy.39) | data formatting | bytes 4194304 | tf_op jit(solution)/shard_map/reshape | solution.py:56
  122.6 4.2 %add.33 = f32[4,128,1024]{2,1,0:T(8,128)} add(f32[4,128,1024]{2,1,0:T(8,128)} %reshape.45, f32[4,128,1024]{2,1,0:T(8,128)} %bitcast.73) | non-fusion elementwise | flops 524288 | bytes 6291456 | tf_op jit(solution)/shard_map/add | solution.py:56
  126.8 0.0 all-to-all-done.2
  126.8 4.8 %all-to-all-start.1 = ((f32[4,128,1024]{2,1,0:T(8,128)}), f32[4,128,1024]{2,1,0:T(8,128)}, u32[]{:S(2)}, u32[]{:S(2)}) async-start(f32[4,128,1024]{2,1,0:T(8,128)} %add.33), calls=%async_computation.1 | async-start | bytes 4194304 | tf_op jit(solution)/shard_map/all_to_all | solution.py:59
  131.6 0.7 reshape.50
  132.3 0.8 slice.15
  133.2 0.8 bitcast_convert_fusion.1
  134.0 2.9 %scatter_fusion.1 = f32[8,128,128]{2,1,0:T(8,128)} fusion(f32[8,128,128]{2,1,0:T(8,128)} %slice.15, s32[8]{0:T(128)S(1)} %fusion.31, f32[8,128,128]{2,1,0:T(8,128)} %bitcast_convert_fusion.1), kind=kCustom, calls=%fused_computation.4 | custom fusion | flops 131072 | bytes 1572896 | tf_op jit(solution)/shard_map/scatter-add | solution.py:90
  136.9 2.0 %copy.45 = f32[8,128,128]{1,2,0:T(8,128)} copy(f32[8,128,128]{2,1,0:T(8,128)} %scatter_fusion.1) | data formatting | bytes 1048576 | tf_op jit(solution)/shard_map/scatter-add | solution.py:90
  138.9 2.3 %fusion.22 = f32[8,128,128]{2,1,0:T(8,128)} fusion(bf16[4,8,128,128]{3,2,1,0:T(8,128)(2,1)S(1)} %bitcast.76, f32[8,128,128]{1,2,0:T(8,128)} %copy.45, bf16[128,4,128,1]{2,1,0,3:T(4,128)(2,1)S(1)} %bitcast.84), kind=kOutput, calls=%fused_computation.24 | convolution fusion | flops 134348800 | bytes 2228224 | tf_op jit(solution)/shard_map/fiae,cfe->iac/dot_general | solution.py:94
  141.3 39.4 %all-to-all-done.1 = f32[4,128,1024]{2,1,0:T(8,128)} async-done(((f32[4,128,1024]{2,1,0:T(8,128)}), f32[4,128,1024]{2,1,0:T(8,128)}, u32[]{:S(2)}, u32[]{:S(2)}) %all-to-all-start.1) | async-done | bytes 2097184 | tf_op jit(solution)/shard_map/all_to_all | solution.py:59
  180.7 1.8 reduce_sum.9
  182.5 0.8 copy.47
  183.4 6.3 %multiply_convert_fusion = bf16[30,128,512]{2,1,0:T(8,128)(2,1)} fusion(f32[30,128,512]{2,1,0:T(8,128)} %all-reduce.2.cloned.1.call-done), kind=kLoop, calls=%fused_computation.12 | loop fusion | flops 3932160 | bytes 11796480 | tf_op jit(solution)/shard_map/convert_element_type | solution.py:52
  (13 shorter events, 0.1 us)
Async XLA Ops:
  7.2 18.1 %copy-start = (bf16[64,128,128]{2,1,0:T(8,128)(2,1)S(1)}, bf16[64,128,128]{2,1,0:T(8,128)(2,1)}, u32[]{:S(2)}) copy-start(bf16[64,128,128]{2,1,0:T(8,128)(2,1)} %param.11) | copy-start | bytes 6291460
  7.2 15.9 %copy-start.2 = (bf16[1024,128]{1,0:T(8,128)(2,1)S(1)}, bf16[1024,128]{1,0:T(8,128)(2,1)}, u32[]{:S(2)}) copy-start(bf16[1024,128]{1,0:T(8,128)(2,1)} %param.10) | copy-start | bytes 786436
  7.2 33.1 %all-gather.3.cloned.1.call-start = ((), (), s32[]{:S(2)}) async-start(), calls=%async_computation.4 | async-start | bytes 1310720 | tf_op jit(solution)/shard_map/all_gather | solution.py:42
  10.8 12.3 %all-to-all-start = ((bf16[8,1,128,128]{2,3,1,0:T(8,128)(2,1)}), bf16[8,1,128,128]{2,3,1,0:T(8,128)(2,1)S(1)}, u32[]{:S(2)}, u32[]{:S(2)}) async-start(bf16[8,1,128,128]{2,3,1,0:T(8,128)(2,1)} %bitcast.6), calls=%async_computation | async-start | bytes 524288 | tf_op jit(solution)/shard_map/all_to_all | solution.py:23
  16.0 167.4 %all-reduce.2.cloned.1.call-start = ((), (), s32[]{:S(2)}) async-start(), calls=%async_computation.3 | async-start | bytes 15728640 | tf_op jit(solution)/shard_map/psum | solution.py:51
  104.6 22.2 %all-to-all-start.2 = ((bf16[8,1,128,128]{3,2,1,0:T(8,128)(2,1)}), bf16[8,1,128,128]{3,2,1,0:T(8,128)(2,1)S(1)}, u32[]{:S(2)}, u32[]{:S(2)}) async-start(bf16[8,1,128,128]{3,2,1,0:T(8,128)(2,1)} %fusion.25), calls=%async_computation.2 | async-start | bytes 524288 | tf_op jit(solution)/shard_map/all_to_all | solution.py:81
  122.6 9.0 %copy-start.3 = (bf16[128,512]{1,0:T(8,128)(2,1)S(1)}, bf16[128,512]{1,0:T(8,128)(2,1)}, u32[]{:S(2)}) copy-start(bf16[128,512]{1,0:T(8,128)(2,1)} %param.18) | copy-start | bytes 393220
  126.8 53.9 %all-to-all-start.1 = ((f32[4,128,1024]{2,1,0:T(8,128)}), f32[4,128,1024]{2,1,0:T(8,128)}, u32[]{:S(2)}, u32[]{:S(2)}) async-start(f32[4,128,1024]{2,1,0:T(8,128)} %add.33), calls=%async_computation.1 | async-start | bytes 4194304 | tf_op jit(solution)/shard_map/all_to_all | solution.py:59
  132.3 6.6 %copy-start.4 = (bf16[128,4,128]{2,1,0:T(4,128)(2,1)S(1)}, bf16[128,4,128]{2,1,0:T(4,128)(2,1)}, u32[]{:S(2)}) copy-start(bf16[128,4,128]{2,1,0:T(4,128)(2,1)} %reshape.50) | copy-start | bytes 393220
  133.2 5.8 %copy-start.1 = (bf16[4096,128]{1,0:T(8,128)(2,1)S(1)}, bf16[4096,128]{1,0:T(8,128)(2,1)}, u32[]{:S(2)}) copy-start(bf16[4096,128]{1,0:T(8,128)(2,1)} %all-gather.3.cloned.1.call-done) | copy-start | bytes 3145732
Sparse Core Ops, SparseCore 0:
  9.6 30.6 all-gather.2
  51.7 123.4 all-reduce.1
